TPU v7x, 256 devices: a whole 4x4x8 slice. The times are simulated.
256 devices in a mesh: dp: 16 (over z, core), tensor: 16 (over y, x).
Axes of the slice: x: 4, y: 4, z: 8, core: 2. Of those that a mesh axis runs over, the one named last changes fastest.
Arguments:
- hidden_rows: bfloat16 [16384, 3584], P(('dp', 'tensor')), parts along dimension 0, may hold values from -48 to 48
- norm_gain: float32 [3584], replicated, may hold values from 0.5 to 2
- gate_weight: bfloat16 [9216, 3584], P('tensor'), may hold values from -0.09375 to 0.09375
- up_weight: bfloat16 [9216, 3584], P('tensor'), may hold values from -0.09375 to 0.09375
- down_weight: bfloat16 [9216, 3584], P('tensor'), may hold values from -0.0625 to 0.0625
- span_lengths: int32 [256], P('dp'), parts along dimension 0, may hold values from 1 to 64, 512 in all
Outputs:
- ffn_out: bfloat16 [16384, 3584], P(('dp', 'tensor')), parts along dimension 0
There are 16 independent parts, one for each index of `dp`. A program takes and returns all parts, laid end to end along the dimension named above; an argument that names none is the same for every part. Nothing has to cross between parts.
Inputs may be any that keep to these rules, and one draw needn't show every extreme that they name: `span_lengths`: the lengths of one part sum to exactly 512, and the largest is exactly 64.
All inputs are finite; a program needn't handle non-finite values.
Results may differ from a plain program's by a relative error of at most 0.0065.
Values may be sent and summed in bfloat16 or wider, within the bound.
No kernel may reach another device: no remote copies, remote signals or barrier semaphores. Data moves between devices by JAX's collectives and lax.ppermute only.
A program may use at most 128 MiB of HBM per device.

v0:
```python
import jax
import jax.numpy as jnp
from jax import lax
from jax.sharding import PartitionSpec as P

NX = 4


def _shift(n, axis, step):
    ny = n // NX
    pairs = []
    for t in range(n):
        y, x = divmod(t, NX)
        if axis == "x":
            d = y * NX + (x + step) % NX
        else:
            d = ((y + step) % ny) * NX + x
        pairs.append((t, d))
    return pairs


def _gather_ring(s, n, axis):
    ahead = lax.ppermute(s, "tensor", _shift(n, axis, -1))
    behind = lax.ppermute(s, "tensor", _shift(n, axis, +1))
    h = s.shape[-2] // 2
    far_lo = lax.ppermute(behind[..., :h, :], "tensor", _shift(n, axis, +1))
    far_hi = lax.ppermute(ahead[..., h:, :], "tensor", _shift(n, axis, -1))
    far = jnp.concatenate([far_lo, far_hi], axis=-2)
    return [s, ahead, far, behind]


def _gather_direct(s, n, axis):
    ahead = lax.ppermute(s, "tensor", _shift(n, axis, -1))
    behind = lax.ppermute(s, "tensor", _shift(n, axis, +1))
    far = lax.ppermute(s, "tensor", _shift(n, axis, +2))
    return [s, ahead, far, behind]


def _reduce_relay(c, n, axis):
    h = c[0].shape[-2] // 2
    lo, hi = (lambda v: v[..., :h, :]), (lambda v: v[..., h:, :])
    bf, f32 = jnp.bfloat16, jnp.float32
    up, down = _shift(n, axis, +1), _shift(n, axis, -1)
    from_behind = lax.ppermute(jnp.concatenate([lo(c[1]), hi(c[2])], axis=-2).astype(bf), "tensor", up)
    from_ahead = lax.ppermute(jnp.concatenate([lo(c[2]), hi(c[3])], axis=-2).astype(bf), "tensor", down)
    relay_up = (hi(c[1]).astype(f32) + hi(from_behind).astype(f32)).astype(bf)
    relay_down = (lo(c[3]).astype(f32) + lo(from_ahead).astype(f32)).astype(bf)
    second_behind = lax.ppermute(relay_up, "tensor", up)
    second_ahead = lax.ppermute(relay_down, "tensor", down)
    own = c[0].astype(f32)
    sum_lo = lo(own) + lo(from_behind).astype(f32) + second_ahead.astype(f32)
    sum_hi = hi(own) + hi(from_ahead).astype(f32) + second_behind.astype(f32)
    return jnp.concatenate([sum_lo, sum_hi], axis=-2)


def _reduce_direct(c, n, axis):
    bf, f32 = jnp.bfloat16, jnp.float32
    from_behind = lax.ppermute(c[1].astype(bf), "tensor", _shift(n, axis, +1))
    from_ahead = lax.ppermute(c[3].astype(bf), "tensor", _shift(n, axis, -1))
    from_far = lax.ppermute(c[2].astype(bf), "tensor", _shift(n, axis, +2))
    return c[0].astype(f32) + from_behind.astype(f32) + from_ahead.astype(f32) + from_far.astype(f32)


def _ffn(rows, gate_weight, up_weight, down_weight):
    dims = (((1,), (1,)), ((), ()))
    gate = lax.dot_general(rows, gate_weight, dims, preferred_element_type=jnp.float32)
    up = lax.dot_general(rows, up_weight, dims, preferred_element_type=jnp.float32)
    act = (jax.nn.silu(gate) * up).astype(jnp.bfloat16)
    act = lax.optimization_barrier(act)
    return jnp.dot(act, down_weight, preferred_element_type=jnp.float32).astype(jnp.bfloat16)


def shards(hidden_rows, norm_gain, gate_weight, up_weight, down_weight, span_lengths):
    capacity, width = hidden_rows.shape
    n = span_lengths.shape[0]
    own_rank = lax.axis_index("tensor")
    widened = hidden_rows.astype(jnp.float32)
    scale = lax.rsqrt(jnp.mean(widened * widened, axis=-1, keepdims=True) + 1e-06)
    normed = (widened * scale * norm_gain).astype(jnp.bfloat16)

    half = capacity // 2

    def ffn(part):
        return _ffn(part.reshape(-1, width), gate_weight, up_weight, down_weight).reshape(part.shape)

    a_x = jnp.stack(_gather_direct(normed[:half], n, "x"))
    b_y = jnp.stack(_gather_direct(normed[half:], n, "y"))
    a0, a1, a2, a3 = _gather_ring(a_x, n, "y")
    b0, b1, b2, b3 = _gather_ring(b_y, n, "x")
    near_a = ffn(jnp.stack([a1, a3]))
    near_b = ffn(jnp.stack([b1, b3]))
    far = ffn(jnp.stack([a2, b2]))
    out_a = [ffn(a0), near_a[0], far[0], near_a[1]]
    out_b = [ffn(b0), near_b[0], far[1], near_b[1]]

    sum_a = _reduce_direct(_reduce_relay(out_a, n, "y"), n, "x")
    sum_b = _reduce_direct(_reduce_relay(out_b, n, "x"), n, "y")
    result = jnp.concatenate([sum_a, sum_b], axis=0).astype(jnp.bfloat16)
    live_mask = jnp.arange(capacity, dtype=jnp.int32) < span_lengths[own_rank]
    return jnp.where(live_mask[:, None], result, jnp.zeros_like(result))


def solution(mesh):
    return jax.shard_map(
        shards,
        mesh=mesh,
        in_specs=(
            P(("dp", "tensor"), None),
            P(),
            P("tensor", None),
            P("tensor", None),
            P("tensor", None),
            P("dp"),
        ),
        out_specs=P(("dp", "tensor"), None),
        check_vma=False,
    )
```

profile of v0, /device:TPU:24, one launch (start us, length us, event | category | flops | bytes accessed | tf_op | source)
XLA Modules:
  0.0 118.0 jit_solution(12449411161524711147)
XLA Ops:
  2.5 2.8 %collective-permute-start = (bf16[32,3584]{1,0:T(8,128)(2,1)S(1)}, bf16[32,3584]{1,0:T(8,128)(2,1)S(1)}, u32[]{:S(2)}, u32[]{:S(2)}) collective-permute-start(bf16[32,3584]{1,0:T(8,128)(2,1)S(1)} %get-tuple-element.28), channel_id=1, source_target_pairs={{0,3},{1,0},{2,1},{3,2},{4,7},{5,4},{6,5},{7,6},{8,11},{9,8},{10,9... | collective-permute-start | bytes 688136 | tf_op jit(solution)/shard_map/ppermute | solution.py:33
  10.0 5.2 %collective-permute-done = bf16[32,3584]{1,0:T(8,128)(2,1)S(1)} collective-permute-done((bf16[32,3584]{1,0:T(8,128)(2,1)S(1)}, bf16[32,3584]{1,0:T(8,128)(2,1)S(1)}, u32[]{:S(2)}, u32[]{:S(2)}) %collective-permute-start) | collective-permute-done | bytes 229408 | tf_op jit(solution)/shard_map/ppermute | solution.py:33
  15.4 3.4 %collective-permute-done.2 = bf16[32,3584]{1,0:T(8,128)(2,1)S(1)} collective-permute-done((bf16[32,3584]{1,0:T(8,128)(2,1)S(1)}, bf16[32,3584]{1,0:T(8,128)(2,1)S(1)}, u32[]{:S(2)}, u32[]{:S(2)}) %collective-permute-start.2) | collective-permute-done | bytes 229408 | tf_op jit(solution)/shard_map/ppermute | solution.py:34
  19.3 1.8 %collective-permute-start.3 = (bf16[4,32,3584]{2,1,0:T(8,128)(2,1)S(1)}, bf16[4,32,3584]{2,1,0:T(8,128)(2,1)S(1)}, u32[]{:S(2)}, u32[]{:S(2)}) collective-permute-start(bf16[4,32,3584]{2,1,0:T(8,128)(2,1)S(1)} %pad_maximum_fusion.5), channel_id=1, source_target_pairs={{0,12},{1,13},{2,14},{3,15},{4,0},{5,1},{6,2},{7,3},{8,4},{9,5},{1... | collective-permute-start | bytes 2752520 | tf_op jit(solution)/shard_map/ppermute | solution.py:23
  21.5 2.8 %collective-permute-start.10 = (bf16[4,32,3584]{2,1,0:T(8,128)(2,1)S(1)}, bf16[4,32,3584]{2,1,0:T(8,128)(2,1)S(1)}, u32[]{:S(2)}, u32[]{:S(2)}) collective-permute-start(bf16[4,32,3584]{2,1,0:T(8,128)(2,1)S(1)} %pad_maximum_fusion.6), channel_id=1, source_target_pairs={{0,1},{1,2},{2,3},{3,0},{4,5},{5,6},{6,7},{7,4},{8,9},{9,10},{10,1... | collective-permute-start | bytes 2752520 | tf_op jit(solution)/shard_map/ppermute | solution.py:24
  24.3 3.3 %collective-permute-start.12 = (bf16[4,32,3584]{2,1,0:T(8,128)(2,1)S(1)}, bf16[4,32,3584]{2,1,0:T(8,128)(2,1)S(1)}, u32[]{:S(2)}, u32[]{:S(2)}) collective-permute-start(bf16[4,32,3584]{2,1,0:T(8,128)(2,1)S(1)} %pad_maximum_fusion.6), channel_id=1, source_target_pairs={{0,3},{1,0},{2,1},{3,2},{4,7},{5,4},{6,5},{7,6},{8,11},{9,8},{10,9... | collective-permute-start | bytes 2752520 | tf_op jit(solution)/shard_map/ppermute | solution.py:23
  27.7 3.5 %fusion.29 = f32[128,576]{0,1:T(8,128)S(1)} fusion(bf16[128,3584]{1,0:T(8,128)(2,1)S(1)} %bitcast.108, bf16[576,3584]{1,0:T(8,128)(2,1)} %param.8), kind=kOutput, calls=%fused_computation.77 | convolution fusion | flops 528482304 | bytes 5341184 | tf_op jit(solution)/shard_map/dot_general | solution.py:66
  39.0 2.3 %collective-permute-done.4 = bf16[4,32,3584]{2,1,0:T(8,128)(2,1)S(1)} collective-permute-done((bf16[4,32,3584]{2,1,0:T(8,128)(2,1)S(1)}, bf16[4,32,3584]{2,1,0:T(8,128)(2,1)S(1)}, u32[]{:S(2)}, u32[]{:S(2)}) %collective-permute-start.4) | collective-permute-done | bytes 917536 | tf_op jit(solution)/shard_map/ppermute | solution.py:24
  41.3 2.7 %collective-permute-start.5 = (bf16[4,16,3584]{2,1,0:T(8,128)(2,1)S(1)}, bf16[4,16,3584]{2,1,0:T(8,128)(2,1)S(1)}, u32[]{:S(2)}, u32[]{:S(2)}) collective-permute-start(bf16[4,16,3584]{2,1,0:T(8,128)(2,1)S(1)} %slice.192), channel_id=1, source_target_pairs={{0,4},{1,5},{2,6},{3,7},{4,8},{5,9},{6,10},{7,11},{8,12},{9,13},{1... | collective-permute-start | bytes 1376264 | tf_op jit(solution)/shard_map/ppermute | solution.py:26
  45.0 2.7 %collective-permute-start.13 = (bf16[4,16,3584]{2,1,0:T(8,128)(2,1)S(1)}, bf16[4,16,3584]{2,1,0:T(8,128)(2,1)S(1)}, u32[]{:S(2)}, u32[]{:S(2)}) collective-permute-start(bf16[4,16,3584]{2,1,0:T(8,128)(2,1)S(1)} %slice.196), channel_id=1, source_target_pairs={{0,3},{1,0},{2,1},{3,2},{4,7},{5,4},{6,5},{7,6},{8,11},{9,8},{10,9... | collective-permute-start | bytes 1376264 | tf_op jit(solution)/shard_map/ppermute | solution.py:27
  50.4 1.6 %convolution_convert_fusion.2 = bf16[256,3584]{1,0:T(8,128)(2,1)S(1)} fusion(bf16[256,576]{0,1:T(8,128)(2,1)S(1)} %multiply_convert_fusion.1, bf16[576,3584]{1,0:T(8,128)(2,1)S(1)} %copy-done), kind=kOutput, calls=%fused_computation.2 | convolution fusion | flops 1057882112 | bytes 6258688 | tf_op jit(solution)/shard_map/dot_general | solution.py:70
  54.9 1.6 %convolution_convert_fusion = bf16[256,3584]{1,0:T(8,128)(2,1)S(1)} fusion(bf16[256,576]{0,1:T(8,128)(2,1)S(1)} %multiply_convert_fusion, bf16[576,3584]{1,0:T(8,128)(2,1)S(1)} %copy-done), kind=kOutput, calls=%fused_computation | convolution fusion | flops 1057882112 | bytes 6258688 | tf_op jit(solution)/shard_map/dot_general | solution.py:70
  59.7 1.6 %convolution_convert_fusion.1 = bf16[256,3584]{1,0:T(8,128)(2,1)S(1)} fusion(bf16[256,576]{0,1:T(8,128)(2,1)S(1)} %fusion.2, bf16[576,3584]{1,0:T(8,128)(2,1)S(1)} %copy-done), kind=kOutput, calls=%fused_computation.1 | convolution fusion | flops 1057882112 | bytes 6258688 | tf_op jit(solution)/shard_map/dot_general | solution.py:70
  62.4 2.9 %collective-permute-start.14 = (bf16[4,32,3584]{2,1,0:T(8,128)(2,1)S(1)}, bf16[4,32,3584]{2,1,0:T(8,128)(2,1)S(1)}, u32[]{:S(2)}, u32[]{:S(2)}) collective-permute-start(bf16[4,32,3584]{2,1,0:T(8,128)(2,1)S(1)} %pad_maximum_fusion.7), channel_id=1, source_target_pairs={{0,4},{1,5},{2,6},{3,7},{4,8},{5,9},{6,10},{7,11},{8,12},{9,13},{1... | collective-permute-start | bytes 2752520 | tf_op jit(solution)/shard_map/ppermute | solution.py:44
  65.4 3.1 %collective-permute-start.22 = (bf16[4,32,3584]{2,1,0:T(8,128)(2,1)S(1)}, bf16[4,32,3584]{2,1,0:T(8,128)(2,1)S(1)}, u32[]{:S(2)}, u32[]{:S(2)}) collective-permute-start(bf16[4,32,3584]{2,1,0:T(8,128)(2,1)S(1)} %pad_maximum_fusion.10), channel_id=1, source_target_pairs={{0,3},{1,0},{2,1},{3,2},{4,7},{5,4},{6,5},{7,6},{8,11},{9,8},{10,9... | collective-permute-start | bytes 2752520 | tf_op jit(solution)/shard_map/ppermute | solution.py:45
  68.7 14.8 %collective-permute-done.15 = bf16[4,32,3584]{2,1,0:T(8,128)(2,1)S(1)} collective-permute-done((bf16[4,32,3584]{2,1,0:T(8,128)(2,1)S(1)}, bf16[4,32,3584]{2,1,0:T(8,128)(2,1)S(1)}, u32[]{:S(2)}, u32[]{:S(2)}) %collective-permute-start.15) | collective-permute-done | bytes 917536 | tf_op jit(solution)/shard_map/ppermute | solution.py:45
  83.8 3.3 %collective-permute-start.17 = (bf16[4,16,3584]{2,1,0:T(8,128)(2,1)S(1)}, bf16[4,16,3584]{2,1,0:T(8,128)(2,1)S(1)}, u32[]{:S(2)}, u32[]{:S(2)}) collective-permute-start(bf16[4,16,3584]{2,1,0:T(8,128)(2,1)S(1)} %add_convert_fusion.2), channel_id=1, source_target_pairs={{0,4},{1,5},{2,6},{3,7},{4,8},{5,9},{6,10},{7,11},{8,12},{9,13},{1... | collective-permute-start | bytes 1376264 | tf_op jit(solution)/shard_map/ppermute | solution.py:48
  87.2 2.5 %collective-permute-start.23 = (bf16[4,16,3584]{2,1,0:T(8,128)(2,1)S(1)}, bf16[4,16,3584]{2,1,0:T(8,128)(2,1)S(1)}, u32[]{:S(2)}, u32[]{:S(2)}) collective-permute-start(bf16[4,16,3584]{2,1,0:T(8,128)(2,1)S(1)} %add_convert_fusion.1), channel_id=1, source_target_pairs={{0,3},{1,0},{2,1},{3,2},{4,7},{5,4},{6,5},{7,6},{8,11},{9,8},{10,9... | collective-permute-start | bytes 1376264 | tf_op jit(solution)/shard_map/ppermute | solution.py:49
  89.9 4.8 %collective-permute-done.16 = bf16[4,16,3584]{2,1,0:T(8,128)(2,1)S(1)} collective-permute-done((bf16[4,16,3584]{2,1,0:T(8,128)(2,1)S(1)}, bf16[4,16,3584]{2,1,0:T(8,128)(2,1)S(1)}, u32[]{:S(2)}, u32[]{:S(2)}) %collective-permute-start.16) | collective-permute-done | bytes 458784 | tf_op jit(solution)/shard_map/ppermute | solution.py:49
  95.6 2.8 %collective-permute-start.19 = (bf16[32,3584]{1,0:T(8,128)(2,1)S(1)}, bf16[32,3584]{1,0:T(8,128)(2,1)S(1)}, u32[]{:S(2)}, u32[]{:S(2)}) collective-permute-start(bf16[32,3584]{1,0:T(8,128)(2,1)S(1)} %get-tuple-element.17), channel_id=1, source_target_pairs={{0,3},{1,0},{2,1},{3,2},{4,7},{5,4},{6,5},{7,6},{8,11},{9,8},{10,9... | collective-permute-start | bytes 688136 | tf_op jit(solution)/shard_map/ppermute | solution.py:59
  98.7 5.5 %collective-permute-done.24 = bf16[4,16,3584]{2,1,0:T(8,128)(2,1)S(1)} collective-permute-done((bf16[4,16,3584]{2,1,0:T(8,128)(2,1)S(1)}, bf16[4,16,3584]{2,1,0:T(8,128)(2,1)S(1)}, u32[]{:S(2)}, u32[]{:S(2)}) %collective-permute-start.24) | collective-permute-done | bytes 458784 | tf_op jit(solution)/shard_map/ppermute | solution.py:48
  106.7 2.7 %collective-permute-done.18 = bf16[32,3584]{1,0:T(8,128)(2,1)S(1)} collective-permute-done((bf16[32,3584]{1,0:T(8,128)(2,1)S(1)}, bf16[32,3584]{1,0:T(8,128)(2,1)S(1)}, u32[]{:S(2)}, u32[]{:S(2)}) %collective-permute-start.18) | collective-permute-done | bytes 229408 | tf_op jit(solution)/shard_map/ppermute | solution.py:58
  110.3 1.9 %collective-permute-done.25 = bf16[32,3584]{1,0:T(8,128)(2,1)S(1)} collective-permute-done((bf16[32,3584]{1,0:T(8,128)(2,1)S(1)}, bf16[32,3584]{1,0:T(8,128)(2,1)S(1)}, u32[]{:S(2)}, u32[]{:S(2)}) %collective-permute-start.25) | collective-permute-done | bytes 229408 | tf_op jit(solution)/shard_map/ppermute | solution.py:58
  113.0 3.9 %collective-permute-done.27 = bf16[32,3584]{1,0:T(8,128)(2,1)S(1)} collective-permute-done((bf16[32,3584]{1,0:T(8,128)(2,1)S(1)}, bf16[32,3584]{1,0:T(8,128)(2,1)S(1)}, u32[]{:S(2)}, u32[]{:S(2)}) %collective-permute-start.27) | collective-permute-done | bytes 229408 | tf_op jit(solution)/shard_map/ppermute | solution.py:60
  (100 shorter events, 33.7 us)
Async XLA Ops:
  2.5 12.6 %collective-permute-start = (bf16[32,3584]{1,0:T(8,128)(2,1)S(1)}, bf16[32,3584]{1,0:T(8,128)(2,1)S(1)}, u32[]{:S(2)}, u32[]{:S(2)}) collective-permute-start(bf16[32,3584]{1,0:T(8,128)(2,1)S(1)} %get-tuple-element.28), channel_id=1, source_target_pairs={{0,3},{1,0},{2,1},{3,2},{4,7},{5,4},{6,5},{7,6},{8,11},{9,8},{10,9... | collective-permute-start | bytes 688136 | tf_op jit(solution)/shard_map/ppermute | solution.py:33
  5.4 10.1 %collective-permute-start.1 = (bf16[32,3584]{1,0:T(8,128)(2,1)S(1)}, bf16[32,3584]{1,0:T(8,128)(2,1)S(1)}, u32[]{:S(2)}, u32[]{:S(2)}) collective-permute-start(bf16[32,3584]{1,0:T(8,128)(2,1)S(1)} %get-tuple-element.28), channel_id=1, source_target_pairs={{0,2},{1,3},{2,0},{3,1},{4,6},{5,7},{6,4},{7,5},{8,10},{9,11},{10,... | collective-permute-start | bytes 688136 | tf_op jit(solution)/shard_map/ppermute | solution.py:35
  6.2 12.7 %collective-permute-start.2 = (bf16[32,3584]{1,0:T(8,128)(2,1)S(1)}, bf16[32,3584]{1,0:T(8,128)(2,1)S(1)}, u32[]{:S(2)}, u32[]{:S(2)}) collective-permute-start(bf16[32,3584]{1,0:T(8,128)(2,1)S(1)} %get-tuple-element.28), channel_id=1, source_target_pairs={{0,1},{1,2},{2,3},{3,0},{4,5},{5,6},{6,7},{7,4},{8,9},{9,10},{10,1... | collective-permute-start | bytes 688136 | tf_op jit(solution)/shard_map/ppermute | solution.py:34
  7.0 14.0 %collective-permute-start.7 = (bf16[32,3584]{1,0:T(8,128)(2,1)S(1)}, bf16[32,3584]{1,0:T(8,128)(2,1)S(1)}, u32[]{:S(2)}, u32[]{:S(2)}) collective-permute-start(bf16[32,3584]{1,0:T(8,128)(2,1)S(1)} %get-tuple-element.27), channel_id=1, source_target_pairs={{0,12},{1,13},{2,14},{3,15},{4,0},{5,1},{6,2},{7,3},{8,4},{9,5},{1... | collective-permute-start | bytes 688136 | tf_op jit(solution)/shard_map/ppermute | solution.py:33
  7.8 13.3 %collective-permute-start.8 = (bf16[32,3584]{1,0:T(8,128)(2,1)S(1)}, bf16[32,3584]{1,0:T(8,128)(2,1)S(1)}, u32[]{:S(2)}, u32[]{:S(2)}) collective-permute-start(bf16[32,3584]{1,0:T(8,128)(2,1)S(1)} %get-tuple-element.27), channel_id=1, source_target_pairs={{0,8},{1,9},{2,10},{3,11},{4,12},{5,13},{6,14},{7,15},{8,0},{9,1},... | collective-permute-start | bytes 688136 | tf_op jit(solution)/shard_map/ppermute | solution.py:35
  19.0 22.3 %collective-permute-start.4 = (bf16[4,32,3584]{2,1,0:T(8,128)(2,1)S(1)}, bf16[4,32,3584]{2,1,0:T(8,128)(2,1)S(1)}, u32[]{:S(2)}, u32[]{:S(2)}) collective-permute-start(bf16[4,32,3584]{2,1,0:T(8,128)(2,1)S(1)} %pad_maximum_fusion.5), channel_id=1, source_target_pairs={{0,4},{1,5},{2,6},{3,7},{4,8},{5,9},{6,10},{7,11},{8,12},{9,13},{1... | collective-permute-start | bytes 2752520 | tf_op jit(solution)/shard_map/ppermute | solution.py:24
  19.3 24.8 %collective-permute-start.3 = (bf16[4,32,3584]{2,1,0:T(8,128)(2,1)S(1)}, bf16[4,32,3584]{2,1,0:T(8,128)(2,1)S(1)}, u32[]{:S(2)}, u32[]{:S(2)}) collective-permute-start(bf16[4,32,3584]{2,1,0:T(8,128)(2,1)S(1)} %pad_maximum_fusion.5), channel_id=1, source_target_pairs={{0,12},{1,13},{2,14},{3,15},{4,0},{5,1},{6,2},{7,3},{8,4},{9,5},{1... | collective-permute-start | bytes 2752520 | tf_op jit(solution)/shard_map/ppermute | solution.py:23
  21.5 22.7 %collective-permute-start.10 = (bf16[4,32,3584]{2,1,0:T(8,128)(2,1)S(1)}, bf16[4,32,3584]{2,1,0:T(8,128)(2,1)S(1)}, u32[]{:S(2)}, u32[]{:S(2)}) collective-permute-start(bf16[4,32,3584]{2,1,0:T(8,128)(2,1)S(1)} %pad_maximum_fusion.6), channel_id=1, source_target_pairs={{0,1},{1,2},{2,3},{3,0},{4,5},{5,6},{6,7},{7,4},{8,9},{9,10},{10,1... | collective-permute-start | bytes 2752520 | tf_op jit(solution)/shard_map/ppermute | solution.py:24
  24.3 20.6 %collective-permute-start.12 = (bf16[4,32,3584]{2,1,0:T(8,128)(2,1)S(1)}, bf16[4,32,3584]{2,1,0:T(8,128)(2,1)S(1)}, u32[]{:S(2)}, u32[]{:S(2)}) collective-permute-start(bf16[4,32,3584]{2,1,0:T(8,128)(2,1)S(1)} %pad_maximum_fusion.6), channel_id=1, source_target_pairs={{0,3},{1,0},{2,1},{3,2},{4,7},{5,4},{6,5},{7,6},{8,11},{9,8},{10,9... | collective-permute-start | bytes 2752520 | tf_op jit(solution)/shard_map/ppermute | solution.py:23
  41.3 15.5 %collective-permute-start.5 = (bf16[4,16,3584]{2,1,0:T(8,128)(2,1)S(1)}, bf16[4,16,3584]{2,1,0:T(8,128)(2,1)S(1)}, u32[]{:S(2)}, u32[]{:S(2)}) collective-permute-start(bf16[4,16,3584]{2,1,0:T(8,128)(2,1)S(1)} %slice.192), channel_id=1, source_target_pairs={{0,4},{1,5},{2,6},{3,7},{4,8},{5,9},{6,10},{7,11},{8,12},{9,13},{1... | collective-permute-start | bytes 1376264 | tf_op jit(solution)/shard_map/ppermute | solution.py:26
  44.1 12.7 %collective-permute-start.6 = (bf16[4,16,3584]{2,1,0:T(8,128)(2,1)S(1)}, bf16[4,16,3584]{2,1,0:T(8,128)(2,1)S(1)}, u32[]{:S(2)}, u32[]{:S(2)}) collective-permute-start(bf16[4,16,3584]{2,1,0:T(8,128)(2,1)S(1)} %slice.193), channel_id=1, source_target_pairs={{0,12},{1,13},{2,14},{3,15},{4,0},{5,1},{6,2},{7,3},{8,4},{9,5},{1... | collective-permute-start | bytes 1376264 | tf_op jit(solution)/shard_map/ppermute | solution.py:27
  44.3 12.6 %collective-permute-start.11 = (bf16[4,16,3584]{2,1,0:T(8,128)(2,1)S(1)}, bf16[4,16,3584]{2,1,0:T(8,128)(2,1)S(1)}, u32[]{:S(2)}, u32[]{:S(2)}) collective-permute-start(bf16[4,16,3584]{2,1,0:T(8,128)(2,1)S(1)} %slice.195), channel_id=1, source_target_pairs={{0,1},{1,2},{2,3},{3,0},{4,5},{5,6},{6,7},{7,4},{8,9},{9,10},{10,1... | collective-permute-start | bytes 1376264 | tf_op jit(solution)/shard_map/ppermute | solution.py:26
  45.0 11.9 %collective-permute-start.13 = (bf16[4,16,3584]{2,1,0:T(8,128)(2,1)S(1)}, bf16[4,16,3584]{2,1,0:T(8,128)(2,1)S(1)}, u32[]{:S(2)}, u32[]{:S(2)}) collective-permute-start(bf16[4,16,3584]{2,1,0:T(8,128)(2,1)S(1)} %slice.196), channel_id=1, source_target_pairs={{0,3},{1,0},{2,1},{3,2},{4,7},{5,4},{6,5},{7,6},{8,11},{9,8},{10,9... | collective-permute-start | bytes 1376264 | tf_op jit(solution)/shard_map/ppermute | solution.py:27
  61.6 21.9 %collective-permute-start.15 = (bf16[4,32,3584]{2,1,0:T(8,128)(2,1)S(1)}, bf16[4,32,3584]{2,1,0:T(8,128)(2,1)S(1)}, u32[]{:S(2)}, u32[]{:S(2)}) collective-permute-start(bf16[4,32,3584]{2,1,0:T(8,128)(2,1)S(1)} %pad_maximum_fusion.8), channel_id=1, source_target_pairs={{0,12},{1,13},{2,14},{3,15},{4,0},{5,1},{6,2},{7,3},{8,4},{9,5},{1... | collective-permute-start | bytes 2752520 | tf_op jit(solution)/shard_map/ppermute | solution.py:45
  62.4 21.3 %collective-permute-start.14 = (bf16[4,32,3584]{2,1,0:T(8,128)(2,1)S(1)}, bf16[4,32,3584]{2,1,0:T(8,128)(2,1)S(1)}, u32[]{:S(2)}, u32[]{:S(2)}) collective-permute-start(bf16[4,32,3584]{2,1,0:T(8,128)(2,1)S(1)} %pad_maximum_fusion.7), channel_id=1, source_target_pairs={{0,4},{1,5},{2,6},{3,7},{4,8},{5,9},{6,10},{7,11},{8,12},{9,13},{1... | collective-permute-start | bytes 2752520 | tf_op jit(solution)/shard_map/ppermute | solution.py:44
  65.4 21.7 %collective-permute-start.22 = (bf16[4,32,3584]{2,1,0:T(8,128)(2,1)S(1)}, bf16[4,32,3584]{2,1,0:T(8,128)(2,1)S(1)}, u32[]{:S(2)}, u32[]{:S(2)}) collective-permute-start(bf16[4,32,3584]{2,1,0:T(8,128)(2,1)S(1)} %pad_maximum_fusion.10), channel_id=1, source_target_pairs={{0,3},{1,0},{2,1},{3,2},{4,7},{5,4},{6,5},{7,6},{8,11},{9,8},{10,9... | collective-permute-start | bytes 2752520 | tf_op jit(solution)/shard_map/ppermute | solution.py:45
  68.6 21.1 %collective-permute-start.21 = (bf16[4,32,3584]{2,1,0:T(8,128)(2,1)S(1)}, bf16[4,32,3584]{2,1,0:T(8,128)(2,1)S(1)}, u32[]{:S(2)}, u32[]{:S(2)}) collective-permute-start(bf16[4,32,3584]{2,1,0:T(8,128)(2,1)S(1)} %pad_maximum_fusion.9), channel_id=1, source_target_pairs={{0,1},{1,2},{2,3},{3,0},{4,5},{5,6},{6,7},{7,4},{8,9},{9,10},{10,1... | collective-permute-start | bytes 2752520 | tf_op jit(solution)/shard_map/ppermute | solution.py:44
  83.6 11.1 %collective-permute-start.16 = (bf16[4,16,3584]{2,1,0:T(8,128)(2,1)S(1)}, bf16[4,16,3584]{2,1,0:T(8,128)(2,1)S(1)}, u32[]{:S(2)}, u32[]{:S(2)}) collective-permute-start(bf16[4,16,3584]{2,1,0:T(8,128)(2,1)S(1)} %add_convert_fusion.3), channel_id=1, source_target_pairs={{0,12},{1,13},{2,14},{3,15},{4,0},{5,1},{6,2},{7,3},{8,4},{9,5},{1... | collective-permute-start | bytes 1376264 | tf_op jit(solution)/shard_map/ppermute | solution.py:49
  83.8 10.9 %collective-permute-start.17 = (bf16[4,16,3584]{2,1,0:T(8,128)(2,1)S(1)}, bf16[4,16,3584]{2,1,0:T(8,128)(2,1)S(1)}, u32[]{:S(2)}, u32[]{:S(2)}) collective-permute-start(bf16[4,16,3584]{2,1,0:T(8,128)(2,1)S(1)} %add_convert_fusion.2), channel_id=1, source_target_pairs={{0,4},{1,5},{2,6},{3,7},{4,8},{5,9},{6,10},{7,11},{8,12},{9,13},{1... | collective-permute-start | bytes 1376264 | tf_op jit(solution)/shard_map/ppermute | solution.py:48
  87.2 11.5 %collective-permute-start.23 = (bf16[4,16,3584]{2,1,0:T(8,128)(2,1)S(1)}, bf16[4,16,3584]{2,1,0:T(8,128)(2,1)S(1)}, u32[]{:S(2)}, u32[]{:S(2)}) collective-permute-start(bf16[4,16,3584]{2,1,0:T(8,128)(2,1)S(1)} %add_convert_fusion.1), channel_id=1, source_target_pairs={{0,3},{1,0},{2,1},{3,2},{4,7},{5,4},{6,5},{7,6},{8,11},{9,8},{10,9... | collective-permute-start | bytes 1376264 | tf_op jit(solution)/shard_map/ppermute | solution.py:49
  89.8 14.4 %collective-permute-start.24 = (bf16[4,16,3584]{2,1,0:T(8,128)(2,1)S(1)}, bf16[4,16,3584]{2,1,0:T(8,128)(2,1)S(1)}, u32[]{:S(2)}, u32[]{:S(2)}) collective-permute-start(bf16[4,16,3584]{2,1,0:T(8,128)(2,1)S(1)} %add_convert_fusion), channel_id=1, source_target_pairs={{0,1},{1,2},{2,3},{3,0},{4,5},{5,6},{6,7},{7,4},{8,9},{9,10},{10,1... | collective-permute-start | bytes 1376264 | tf_op jit(solution)/shard_map/ppermute | solution.py:48
  95.1 14.3 %collective-permute-start.18 = (bf16[32,3584]{1,0:T(8,128)(2,1)S(1)}, bf16[32,3584]{1,0:T(8,128)(2,1)S(1)}, u32[]{:S(2)}, u32[]{:S(2)}) collective-permute-start(bf16[32,3584]{1,0:T(8,128)(2,1)S(1)} %get-tuple-element.15), channel_id=1, source_target_pairs={{0,1},{1,2},{2,3},{3,0},{4,5},{5,6},{6,7},{7,4},{8,9},{9,10},{10,1... | collective-permute-start | bytes 688136 | tf_op jit(solution)/shard_map/ppermute | solution.py:58
  95.6 14.6 %collective-permute-start.19 = (bf16[32,3584]{1,0:T(8,128)(2,1)S(1)}, bf16[32,3584]{1,0:T(8,128)(2,1)S(1)}, u32[]{:S(2)}, u32[]{:S(2)}) collective-permute-start(bf16[32,3584]{1,0:T(8,128)(2,1)S(1)} %get-tuple-element.17), channel_id=1, source_target_pairs={{0,3},{1,0},{2,1},{3,2},{4,7},{5,4},{6,5},{7,6},{8,11},{9,8},{10,9... | collective-permute-start | bytes 688136 | tf_op jit(solution)/shard_map/ppermute | solution.py:59
  98.4 11.8 %collective-permute-start.20 = (bf16[32,3584]{1,0:T(8,128)(2,1)S(1)}, bf16[32,3584]{1,0:T(8,128)(2,1)S(1)}, u32[]{:S(2)}, u32[]{:S(2)}) collective-permute-start(bf16[32,3584]{1,0:T(8,128)(2,1)S(1)} %get-tuple-element.16), channel_id=1, source_target_pairs={{0,2},{1,3},{2,0},{3,1},{4,6},{5,7},{6,4},{7,5},{8,10},{9,11},{10,... | collective-permute-start | bytes 688136 | tf_op jit(solution)/shard_map/ppermute | solution.py:60
  (8 other events, 45.2 us)
where the time goes:
time: 118 us
  waiting for transfers between devices  46 us (39%)
  starting transfers between devices  39.9 us (34%)
  matrix products  21.5 us (18%)
  other arithmetic  6.79 us (6%)
  local copies, waits for them, and re-layouts  3.36 us (3%)
    ppermute x2, waiting for transfers between devices, _reduce_relay(): lax.ppermute(jnp.concatenate([lo(c[2]), hi(c[3])], axis=-2).astype(bf), '...  14.8 us
    dot_general x5, matrix products, _ffn(): lax.dot_general(rows, gate_weight, dims, preferred_element_type=jnp.float32)  8.55 us
    dot_general x5, matrix products, _ffn(): jnp.dot(act, down_weight, preferred_element_type=jnp.float32)  6.65 us
    dot_general x5, matrix products, _ffn(): lax.dot_general(rows, up_weight, dims, preferred_element_type=jnp.float32)  6.27 us
    ppermute x2, waiting for transfers between devices, _reduce_relay(): second_behind = lax.ppermute(relay_up, 'tensor', up)  5.53 us
    ppermute x2, waiting for transfers between devices, _gather_direct(): ahead = lax.ppermute(s, 'tensor', _shift(n, axis, -1))  5.2 us
    ppermute x2, starting transfers between devices, _gather_ring(): ahead = lax.ppermute(s, 'tensor', _shift(n, axis, -1))  5.15 us
    ppermute x2, waiting for transfers between devices, _reduce_relay(): second_ahead = lax.ppermute(relay_down, 'tensor', down)  4.98 us
  transfers between devices with their start and end apart: 28, of which 13 were waited for; matrix products, arithmetic and copies ran while one was open for 18% of the time, Pallas kernels for 0%

commit v1 on v0

--- a/solution.py
+++ b/solution.py
@@ -90,8 +90,9 @@
     near_a = ffn(jnp.stack([a1, a3]))
     near_b = ffn(jnp.stack([b1, b3]))
     far = ffn(jnp.stack([a2, b2]))
-    out_a = [ffn(a0), near_a[0], far[0], near_a[1]]
-    out_b = [ffn(b0), near_b[0], far[1], near_b[1]]
+    own = ffn(jnp.stack([a0, b0]))
+    out_a = [own[0], near_a[0], far[0], near_a[1]]
+    out_b = [own[1], near_b[0], far[1], near_b[1]]
 
     sum_a = _reduce_direct(_reduce_relay(out_a, n, "y"), n, "x")
     sum_b = _reduce_direct(_reduce_relay(out_b, n, "x"), n, "y")

time: 118 us -> 118 us (level)
  matrix products: 21.5 us -> 16.6 us
  waiting for transfers between devices: 46 us -> 50.6 us
    ppermute x2, waiting for transfers between devices: 2.34 us -> 7.08 us  [_gather_ring(): behind = lax.ppermute(s, 'tensor', _shift(n, axis, +1))]
    dot_general x5 -> x4, matrix products: 8.55 us -> 5.04 us  [_ffn(): lax.dot_general(rows, gate_weight, dims, preferred_element_type=jnp.float32)]
    dot_general x5 -> x4, matrix products: 6.27 us -> 5.08 us  [_ffn(): lax.dot_general(rows, up_weight, dims, preferred_element_type=jnp.float32)]
    dot_general x5 -> x4, matrix products: 6.65 us -> 6.45 us  [_ffn(): jnp.dot(act, down_weight, preferred_element_type=jnp.float32)]
  transfers between devices with their start and end apart: 28 -> 28, of which waited for: 13 -> 14; matrix products, arithmetic and copies ran while one was open for 18% -> 14% of each run, Pallas kernels for 0% -> 0%
where the time goes in v1:
time: 118 us
  waiting for transfers between devices  50.6 us (43%)
  starting transfers between devices  39.9 us (34%)
  matrix products  16.6 us (14%)
  other arithmetic  7.04 us (6%)
  local copies, waits for them, and re-layouts  3.38 us (3%)
    ppermute x2, waiting for transfers between devices, _reduce_relay(): lax.ppermute(jnp.concatenate([lo(c[2]), hi(c[3])], axis=-2).astype(bf), '...  14.8 us
    ppermute x2, waiting for transfers between devices, _gather_ring(): behind = lax.ppermute(s, 'tensor', _shift(n, axis, +1))  7.08 us
    dot_general x4, matrix products, _ffn(): jnp.dot(act, down_weight, preferred_element_type=jnp.float32)  6.45 us
    ppermute x2, waiting for transfers between devices, _reduce_relay(): second_behind = lax.ppermute(relay_up, 'tensor', up)  5.55 us
    ppermute x2, waiting for transfers between devices, _gather_direct(): ahead = lax.ppermute(s, 'tensor', _shift(n, axis, -1))  5.2 us
    ppermute x2, starting transfers between devices, _gather_ring(): ahead = lax.ppermute(s, 'tensor', _shift(n, axis, -1))  5.18 us
    dot_general x4, matrix products, _ffn(): lax.dot_general(rows, up_weight, dims, preferred_element_type=jnp.float32)  5.08 us
    ppermute x2, waiting for transfers between devices, _reduce_relay(): second_ahead = lax.ppermute(relay_down, 'tensor', down)  5.05 us
  transfers between devices with their start and end apart: 28, of which 14 were waited for; matrix products, arithmetic and copies ran while one was open for 14% of the time, Pallas kernels for 0%

profile of v1, /device:TPU:24, one launch (start us, length us, event | category | flops | bytes accessed | tf_op | source)
XLA Modules:
  0.0 118.0 jit_solution(5915949244562638100)
XLA Ops:
  2.5 2.8 %collective-permute-start = (bf16[32,3584]{1,0:T(8,128)(2,1)S(1)}, bf16[32,3584]{1,0:T(8,128)(2,1)S(1)}, u32[]{:S(2)}, u32[]{:S(2)}) collective-permute-start(bf16[32,3584]{1,0:T(8,128)(2,1)S(1)} %get-tuple-element.34), channel_id=1, source_target_pairs={{0,3},{1,0},{2,1},{3,2},{4,7},{5,4},{6,5},{7,6},{8,11},{9,8},{10,9... | collective-permute-start | bytes 688136 | tf_op jit(solution)/shard_map/ppermute | solution.py:33
  10.0 5.2 %collective-permute-done = bf16[32,3584]{1,0:T(8,128)(2,1)S(1)} collective-permute-done((bf16[32,3584]{1,0:T(8,128)(2,1)S(1)}, bf16[32,3584]{1,0:T(8,128)(2,1)S(1)}, u32[]{:S(2)}, u32[]{:S(2)}) %collective-permute-start) | collective-permute-done | bytes 229408 | tf_op jit(solution)/shard_map/ppermute | solution.py:33
  15.4 3.4 %collective-permute-done.2 = bf16[32,3584]{1,0:T(8,128)(2,1)S(1)} collective-permute-done((bf16[32,3584]{1,0:T(8,128)(2,1)S(1)}, bf16[32,3584]{1,0:T(8,128)(2,1)S(1)}, u32[]{:S(2)}, u32[]{:S(2)}) %collective-permute-start.2) | collective-permute-done | bytes 229408 | tf_op jit(solution)/shard_map/ppermute | solution.py:34
  19.3 1.8 %collective-permute-start.6 = (bf16[4,32,3584]{2,1,0:T(8,128)(2,1)S(1)}, bf16[4,32,3584]{2,1,0:T(8,128)(2,1)S(1)}, u32[]{:S(2)}, u32[]{:S(2)}) collective-permute-start(bf16[4,32,3584]{2,1,0:T(8,128)(2,1)S(1)} %get-tuple-element.27), channel_id=1, source_target_pairs={{0,12},{1,13},{2,14},{3,15},{4,0},{5,1},{6,2},{7,3},{8,4},{9,5},{1... | collective-permute-start | bytes 2752520 | tf_op jit(solution)/shard_map/ppermute | solution.py:23
  21.5 2.8 %collective-permute-start.10 = (bf16[4,32,3584]{2,1,0:T(8,128)(2,1)S(1)}, bf16[4,32,3584]{2,1,0:T(8,128)(2,1)S(1)}, u32[]{:S(2)}, u32[]{:S(2)}) collective-permute-start(bf16[4,32,3584]{2,1,0:T(8,128)(2,1)S(1)} %get-tuple-element.29), channel_id=1, source_target_pairs={{0,1},{1,2},{2,3},{3,0},{4,5},{5,6},{6,7},{7,4},{8,9},{9,10},{10,1... | collective-permute-start | bytes 2752520 | tf_op jit(solution)/shard_map/ppermute | solution.py:24
  24.3 3.4 %collective-permute-start.12 = (bf16[4,32,3584]{2,1,0:T(8,128)(2,1)S(1)}, bf16[4,32,3584]{2,1,0:T(8,128)(2,1)S(1)}, u32[]{:S(2)}, u32[]{:S(2)}) collective-permute-start(bf16[4,32,3584]{2,1,0:T(8,128)(2,1)S(1)} %get-tuple-element.29), channel_id=1, source_target_pairs={{0,3},{1,0},{2,1},{3,2},{4,7},{5,4},{6,5},{7,6},{8,11},{9,8},{10,9... | collective-permute-start | bytes 2752520 | tf_op jit(solution)/shard_map/ppermute | solution.py:23
  32.2 1.6 %convolution_convert_fusion.3 = bf16[256,3584]{1,0:T(8,128)(2,1)S(1)} fusion(bf16[256,576]{0,1:T(8,128)(2,1)S(1)} %fusion.2, bf16[576,3584]{1,0:T(8,128)(2,1)S(1)} %copy-done), kind=kOutput, calls=%fused_computation.3 | convolution fusion | flops 1057882112 | bytes 6258688 | tf_op jit(solution)/shard_map/dot_general | solution.py:70
  34.3 7.0 %collective-permute-done.7 = bf16[4,32,3584]{2,1,0:T(8,128)(2,1)S(1)} collective-permute-done((bf16[4,32,3584]{2,1,0:T(8,128)(2,1)S(1)}, bf16[4,32,3584]{2,1,0:T(8,128)(2,1)S(1)}, u32[]{:S(2)}, u32[]{:S(2)}) %collective-permute-start.7) | collective-permute-done | bytes 917536 | tf_op jit(solution)/shard_map/ppermute | solution.py:24
  41.4 2.5 %collective-permute-start.8 = (bf16[4,16,3584]{2,1,0:T(8,128)(2,1)S(1)}, bf16[4,16,3584]{2,1,0:T(8,128)(2,1)S(1)}, u32[]{:S(2)}, u32[]{:S(2)}) collective-permute-start(bf16[4,16,3584]{2,1,0:T(8,128)(2,1)S(1)} %slice.204), channel_id=1, source_target_pairs={{0,4},{1,5},{2,6},{3,7},{4,8},{5,9},{6,10},{7,11},{8,12},{9,13},{1... | collective-permute-start | bytes 1376264 | tf_op jit(solution)/shard_map/ppermute | solution.py:26
  45.0 2.8 %collective-permute-start.13 = (bf16[4,16,3584]{2,1,0:T(8,128)(2,1)S(1)}, bf16[4,16,3584]{2,1,0:T(8,128)(2,1)S(1)}, u32[]{:S(2)}, u32[]{:S(2)}) collective-permute-start(bf16[4,16,3584]{2,1,0:T(8,128)(2,1)S(1)} %slice.207), channel_id=1, source_target_pairs={{0,3},{1,0},{2,1},{3,2},{4,7},{5,4},{6,5},{7,6},{8,11},{9,8},{10,9... | collective-permute-start | bytes 1376264 | tf_op jit(solution)/shard_map/ppermute | solution.py:27
  50.5 1.6 %convolution_convert_fusion.2 = bf16[256,3584]{1,0:T(8,128)(2,1)S(1)} fusion(bf16[256,576]{0,1:T(8,128)(2,1)S(1)} %multiply_convert_fusion.1, bf16[576,3584]{1,0:T(8,128)(2,1)S(1)} %copy-done), kind=kOutput, calls=%fused_computation.2 | convolution fusion | flops 1057882112 | bytes 6258688 | tf_op jit(solution)/shard_map/dot_general | solution.py:70
  54.9 1.6 %convolution_convert_fusion = bf16[256,3584]{1,0:T(8,128)(2,1)S(1)} fusion(bf16[256,576]{0,1:T(8,128)(2,1)S(1)} %multiply_convert_fusion, bf16[576,3584]{1,0:T(8,128)(2,1)S(1)} %copy-done), kind=kOutput, calls=%fused_computation | convolution fusion | flops 1057882112 | bytes 6258688 | tf_op jit(solution)/shard_map/dot_general | solution.py:70
  59.7 1.6 %convolution_convert_fusion.1 = bf16[256,3584]{1,0:T(8,128)(2,1)S(1)} fusion(bf16[256,576]{0,1:T(8,128)(2,1)S(1)} %fusion.3, bf16[576,3584]{1,0:T(8,128)(2,1)S(1)} %copy-done), kind=kOutput, calls=%fused_computation.1 | convolution fusion | flops 1057882112 | bytes 6258688 | tf_op jit(solution)/shard_map/dot_general | solution.py:70
  62.5 2.8 %collective-permute-start.14 = (bf16[4,32,3584]{2,1,0:T(8,128)(2,1)S(1)}, bf16[4,32,3584]{2,1,0:T(8,128)(2,1)S(1)}, u32[]{:S(2)}, u32[]{:S(2)}) collective-permute-start(bf16[4,32,3584]{2,1,0:T(8,128)(2,1)S(1)} %pad_maximum_fusion.8), channel_id=1, source_target_pairs={{0,4},{1,5},{2,6},{3,7},{4,8},{5,9},{6,10},{7,11},{8,12},{9,13},{1... | collective-permute-start | bytes 2752520 | tf_op jit(solution)/shard_map/ppermute | solution.py:44
  65.4 3.1 %collective-permute-start.22 = (bf16[4,32,3584]{2,1,0:T(8,128)(2,1)S(1)}, bf16[4,32,3584]{2,1,0:T(8,128)(2,1)S(1)}, u32[]{:S(2)}, u32[]{:S(2)}) collective-permute-start(bf16[4,32,3584]{2,1,0:T(8,128)(2,1)S(1)} %pad_maximum_fusion.11), channel_id=1, source_target_pairs={{0,3},{1,0},{2,1},{3,2},{4,7},{5,4},{6,5},{7,6},{8,11},{9,8},{10,9... | collective-permute-start | bytes 2752520 | tf_op jit(solution)/shard_map/ppermute | solution.py:45
  68.7 14.8 %collective-permute-done.15 = bf16[4,32,3584]{2,1,0:T(8,128)(2,1)S(1)} collective-permute-done((bf16[4,32,3584]{2,1,0:T(8,128)(2,1)S(1)}, bf16[4,32,3584]{2,1,0:T(8,128)(2,1)S(1)}, u32[]{:S(2)}, u32[]{:S(2)}) %collective-permute-start.15) | collective-permute-done | bytes 917536 | tf_op jit(solution)/shard_map/ppermute | solution.py:45
  83.8 3.3 %collective-permute-start.17 = (bf16[4,16,3584]{2,1,0:T(8,128)(2,1)S(1)}, bf16[4,16,3584]{2,1,0:T(8,128)(2,1)S(1)}, u32[]{:S(2)}, u32[]{:S(2)}) collective-permute-start(bf16[4,16,3584]{2,1,0:T(8,128)(2,1)S(1)} %add_convert_fusion.2), channel_id=1, source_target_pairs={{0,4},{1,5},{2,6},{3,7},{4,8},{5,9},{6,10},{7,11},{8,12},{9,13},{1... | collective-permute-start | bytes 1376264 | tf_op jit(solution)/shard_map/ppermute | solution.py:48
  87.2 2.5 %collective-permute-start.23 = (bf16[4,16,3584]{2,1,0:T(8,128)(2,1)S(1)}, bf16[4,16,3584]{2,1,0:T(8,128)(2,1)S(1)}, u32[]{:S(2)}, u32[]{:S(2)}) collective-permute-start(bf16[4,16,3584]{2,1,0:T(8,128)(2,1)S(1)} %add_convert_fusion.1), channel_id=1, source_target_pairs={{0,3},{1,0},{2,1},{3,2},{4,7},{5,4},{6,5},{7,6},{8,11},{9,8},{10,9... | collective-permute-start | bytes 1376264 | tf_op jit(solution)/shard_map/ppermute | solution.py:49
  89.9 4.8 %collective-permute-done.16 = bf16[4,16,3584]{2,1,0:T(8,128)(2,1)S(1)} collective-permute-done((bf16[4,16,3584]{2,1,0:T(8,128)(2,1)S(1)}, bf16[4,16,3584]{2,1,0:T(8,128)(2,1)S(1)}, u32[]{:S(2)}, u32[]{:S(2)}) %collective-permute-start.16) | collective-permute-done | bytes 458784 | tf_op jit(solution)/shard_map/ppermute | solution.py:49
  95.6 2.9 %collective-permute-start.19 = (bf16[32,3584]{1,0:T(8,128)(2,1)S(1)}, bf16[32,3584]{1,0:T(8,128)(2,1)S(1)}, u32[]{:S(2)}, u32[]{:S(2)}) collective-permute-start(bf16[32,3584]{1,0:T(8,128)(2,1)S(1)} %get-tuple-element.19), channel_id=1, source_target_pairs={{0,3},{1,0},{2,1},{3,2},{4,7},{5,4},{6,5},{7,6},{8,11},{9,8},{10,9... | collective-permute-start | bytes 688136 | tf_op jit(solution)/shard_map/ppermute | solution.py:59
  98.7 5.5 %collective-permute-done.24 = bf16[4,16,3584]{2,1,0:T(8,128)(2,1)S(1)} collective-permute-done((bf16[4,16,3584]{2,1,0:T(8,128)(2,1)S(1)}, bf16[4,16,3584]{2,1,0:T(8,128)(2,1)S(1)}, u32[]{:S(2)}, u32[]{:S(2)}) %collective-permute-start.24) | collective-permute-done | bytes 458784 | tf_op jit(solution)/shard_map/ppermute | solution.py:48
  106.8 2.6 %collective-permute-done.18 = bf16[32,3584]{1,0:T(8,128)(2,1)S(1)} collective-permute-done((bf16[32,3584]{1,0:T(8,128)(2,1)S(1)}, bf16[32,3584]{1,0:T(8,128)(2,1)S(1)}, u32[]{:S(2)}, u32[]{:S(2)}) %collective-permute-start.18) | collective-permute-done | bytes 229408 | tf_op jit(solution)/shard_map/ppermute | solution.py:58
  110.4 1.9 %collective-permute-done.25 = bf16[32,3584]{1,0:T(8,128)(2,1)S(1)} collective-permute-done((bf16[32,3584]{1,0:T(8,128)(2,1)S(1)}, bf16[32,3584]{1,0:T(8,128)(2,1)S(1)}, u32[]{:S(2)}, u32[]{:S(2)}) %collective-permute-start.25) | collective-permute-done | bytes 229408 | tf_op jit(solution)/shard_map/ppermute | solution.py:58
  113.1 3.8 %collective-permute-done.27 = bf16[32,3584]{1,0:T(8,128)(2,1)S(1)} collective-permute-done((bf16[32,3584]{1,0:T(8,128)(2,1)S(1)}, bf16[32,3584]{1,0:T(8,128)(2,1)S(1)}, u32[]{:S(2)}, u32[]{:S(2)}) %collective-permute-start.27) | collective-permute-done | bytes 229408 | tf_op jit(solution)/shard_map/ppermute | solution.py:60
  (99 shorter events, 31.2 us)
Async XLA Ops:
  2.5 12.6 %collective-permute-start = (bf16[32,3584]{1,0:T(8,128)(2,1)S(1)}, bf16[32,3584]{1,0:T(8,128)(2,1)S(1)}, u32[]{:S(2)}, u32[]{:S(2)}) collective-permute-start(bf16[32,3584]{1,0:T(8,128)(2,1)S(1)} %get-tuple-element.34), channel_id=1, source_target_pairs={{0,3},{1,0},{2,1},{3,2},{4,7},{5,4},{6,5},{7,6},{8,11},{9,8},{10,9... | collective-permute-start | bytes 688136 | tf_op jit(solution)/shard_map/ppermute | solution.py:33
  5.4 10.1 %collective-permute-start.1 = (bf16[32,3584]{1,0:T(8,128)(2,1)S(1)}, bf16[32,3584]{1,0:T(8,128)(2,1)S(1)}, u32[]{:S(2)}, u32[]{:S(2)}) collective-permute-start(bf16[32,3584]{1,0:T(8,128)(2,1)S(1)} %get-tuple-element.34), channel_id=1, source_target_pairs={{0,2},{1,3},{2,0},{3,1},{4,6},{5,7},{6,4},{7,5},{8,10},{9,11},{10,... | collective-permute-start | bytes 688136 | tf_op jit(solution)/shard_map/ppermute | solution.py:35
  6.2 12.7 %collective-permute-start.2 = (bf16[32,3584]{1,0:T(8,128)(2,1)S(1)}, bf16[32,3584]{1,0:T(8,128)(2,1)S(1)}, u32[]{:S(2)}, u32[]{:S(2)}) collective-permute-start(bf16[32,3584]{1,0:T(8,128)(2,1)S(1)} %get-tuple-element.34), channel_id=1, source_target_pairs={{0,1},{1,2},{2,3},{3,0},{4,5},{5,6},{6,7},{7,4},{8,9},{9,10},{10,1... | collective-permute-start | bytes 688136 | tf_op jit(solution)/shard_map/ppermute | solution.py:34
  7.0 14.1 %collective-permute-start.3 = (bf16[32,3584]{1,0:T(8,128)(2,1)S(1)}, bf16[32,3584]{1,0:T(8,128)(2,1)S(1)}, u32[]{:S(2)}, u32[]{:S(2)}) collective-permute-start(bf16[32,3584]{1,0:T(8,128)(2,1)S(1)} %get-tuple-element.33), channel_id=1, source_target_pairs={{0,12},{1,13},{2,14},{3,15},{4,0},{5,1},{6,2},{7,3},{8,4},{9,5},{1... | collective-permute-start | bytes 688136 | tf_op jit(solution)/shard_map/ppermute | solution.py:33
  7.8 13.3 %collective-permute-start.4 = (bf16[32,3584]{1,0:T(8,128)(2,1)S(1)}, bf16[32,3584]{1,0:T(8,128)(2,1)S(1)}, u32[]{:S(2)}, u32[]{:S(2)}) collective-permute-start(bf16[32,3584]{1,0:T(8,128)(2,1)S(1)} %get-tuple-element.33), channel_id=1, source_target_pairs={{0,8},{1,9},{2,10},{3,11},{4,12},{5,13},{6,14},{7,15},{8,0},{9,1},... | collective-permute-start | bytes 688136 | tf_op jit(solution)/shard_map/ppermute | solution.py:35
  19.0 22.3 %collective-permute-start.7 = (bf16[4,32,3584]{2,1,0:T(8,128)(2,1)S(1)}, bf16[4,32,3584]{2,1,0:T(8,128)(2,1)S(1)}, u32[]{:S(2)}, u32[]{:S(2)}) collective-permute-start(bf16[4,32,3584]{2,1,0:T(8,128)(2,1)S(1)} %get-tuple-element.27), channel_id=1, source_target_pairs={{0,4},{1,5},{2,6},{3,7},{4,8},{5,9},{6,10},{7,11},{8,12},{9,13},{1... | collective-permute-start | bytes 2752520 | tf_op jit(solution)/shard_map/ppermute | solution.py:24
  19.3 24.6 %collective-permute-start.6 = (bf16[4,32,3584]{2,1,0:T(8,128)(2,1)S(1)}, bf16[4,32,3584]{2,1,0:T(8,128)(2,1)S(1)}, u32[]{:S(2)}, u32[]{:S(2)}) collective-permute-start(bf16[4,32,3584]{2,1,0:T(8,128)(2,1)S(1)} %get-tuple-element.27), channel_id=1, source_target_pairs={{0,12},{1,13},{2,14},{3,15},{4,0},{5,1},{6,2},{7,3},{8,4},{9,5},{1... | collective-permute-start | bytes 2752520 | tf_op jit(solution)/shard_map/ppermute | solution.py:23
  21.5 22.8 %collective-permute-start.10 = (bf16[4,32,3584]{2,1,0:T(8,128)(2,1)S(1)}, bf16[4,32,3584]{2,1,0:T(8,128)(2,1)S(1)}, u32[]{:S(2)}, u32[]{:S(2)}) collective-permute-start(bf16[4,32,3584]{2,1,0:T(8,128)(2,1)S(1)} %get-tuple-element.29), channel_id=1, source_target_pairs={{0,1},{1,2},{2,3},{3,0},{4,5},{5,6},{6,7},{7,4},{8,9},{9,10},{10,1... | collective-permute-start | bytes 2752520 | tf_op jit(solution)/shard_map/ppermute | solution.py:24
  24.3 20.6 %collective-permute-start.12 = (bf16[4,32,3584]{2,1,0:T(8,128)(2,1)S(1)}, bf16[4,32,3584]{2,1,0:T(8,128)(2,1)S(1)}, u32[]{:S(2)}, u32[]{:S(2)}) collective-permute-start(bf16[4,32,3584]{2,1,0:T(8,128)(2,1)S(1)} %get-tuple-element.29), channel_id=1, source_target_pairs={{0,3},{1,0},{2,1},{3,2},{4,7},{5,4},{6,5},{7,6},{8,11},{9,8},{10,9... | collective-permute-start | bytes 2752520 | tf_op jit(solution)/shard_map/ppermute | solution.py:23
  41.4 15.5 %collective-permute-start.8 = (bf16[4,16,3584]{2,1,0:T(8,128)(2,1)S(1)}, bf16[4,16,3584]{2,1,0:T(8,128)(2,1)S(1)}, u32[]{:S(2)}, u32[]{:S(2)}) collective-permute-start(bf16[4,16,3584]{2,1,0:T(8,128)(2,1)S(1)} %slice.204), channel_id=1, source_target_pairs={{0,4},{1,5},{2,6},{3,7},{4,8},{5,9},{6,10},{7,11},{8,12},{9,13},{1... | collective-permute-start | bytes 1376264 | tf_op jit(solution)/shard_map/ppermute | solution.py:26
  43.9 12.9 %collective-permute-start.9 = (bf16[4,16,3584]{2,1,0:T(8,128)(2,1)S(1)}, bf16[4,16,3584]{2,1,0:T(8,128)(2,1)S(1)}, u32[]{:S(2)}, u32[]{:S(2)}) collective-permute-start(bf16[4,16,3584]{2,1,0:T(8,128)(2,1)S(1)} %slice.205), channel_id=1, source_target_pairs={{0,12},{1,13},{2,14},{3,15},{4,0},{5,1},{6,2},{7,3},{8,4},{9,5},{1... | collective-permute-start | bytes 1376264 | tf_op jit(solution)/shard_map/ppermute | solution.py:27
  44.3 12.6 %collective-permute-start.11 = (bf16[4,16,3584]{2,1,0:T(8,128)(2,1)S(1)}, bf16[4,16,3584]{2,1,0:T(8,128)(2,1)S(1)}, u32[]{:S(2)}, u32[]{:S(2)}) collective-permute-start(bf16[4,16,3584]{2,1,0:T(8,128)(2,1)S(1)} %slice.206), channel_id=1, source_target_pairs={{0,1},{1,2},{2,3},{3,0},{4,5},{5,6},{6,7},{7,4},{8,9},{9,10},{10,1... | collective-permute-start | bytes 1376264 | tf_op jit(solution)/shard_map/ppermute | solution.py:26
  45.0 12.0 %collective-permute-start.13 = (bf16[4,16,3584]{2,1,0:T(8,128)(2,1)S(1)}, bf16[4,16,3584]{2,1,0:T(8,128)(2,1)S(1)}, u32[]{:S(2)}, u32[]{:S(2)}) collective-permute-start(bf16[4,16,3584]{2,1,0:T(8,128)(2,1)S(1)} %slice.207), channel_id=1, source_target_pairs={{0,3},{1,0},{2,1},{3,2},{4,7},{5,4},{6,5},{7,6},{8,11},{9,8},{10,9... | collective-permute-start | bytes 1376264 | tf_op jit(solution)/shard_map/ppermute | solution.py:27
  61.6 21.9 %collective-permute-start.15 = (bf16[4,32,3584]{2,1,0:T(8,128)(2,1)S(1)}, bf16[4,32,3584]{2,1,0:T(8,128)(2,1)S(1)}, u32[]{:S(2)}, u32[]{:S(2)}) collective-permute-start(bf16[4,32,3584]{2,1,0:T(8,128)(2,1)S(1)} %pad_maximum_fusion.9), channel_id=1, source_target_pairs={{0,12},{1,13},{2,14},{3,15},{4,0},{5,1},{6,2},{7,3},{8,4},{9,5},{1... | collective-permute-start | bytes 2752520 | tf_op jit(solution)/shard_map/ppermute | solution.py:45
  62.5 21.2 %collective-permute-start.14 = (bf16[4,32,3584]{2,1,0:T(8,128)(2,1)S(1)}, bf16[4,32,3584]{2,1,0:T(8,128)(2,1)S(1)}, u32[]{:S(2)}, u32[]{:S(2)}) collective-permute-start(bf16[4,32,3584]{2,1,0:T(8,128)(2,1)S(1)} %pad_maximum_fusion.8), channel_id=1, source_target_pairs={{0,4},{1,5},{2,6},{3,7},{4,8},{5,9},{6,10},{7,11},{8,12},{9,13},{1... | collective-permute-start | bytes 2752520 | tf_op jit(solution)/shard_map/ppermute | solution.py:44
  65.4 21.7 %collective-permute-start.22 = (bf16[4,32,3584]{2,1,0:T(8,128)(2,1)S(1)}, bf16[4,32,3584]{2,1,0:T(8,128)(2,1)S(1)}, u32[]{:S(2)}, u32[]{:S(2)}) collective-permute-start(bf16[4,32,3584]{2,1,0:T(8,128)(2,1)S(1)} %pad_maximum_fusion.11), channel_id=1, source_target_pairs={{0,3},{1,0},{2,1},{3,2},{4,7},{5,4},{6,5},{7,6},{8,11},{9,8},{10,9... | collective-permute-start | bytes 2752520 | tf_op jit(solution)/shard_map/ppermute | solution.py:45
  68.6 21.1 %collective-permute-start.21 = (bf16[4,32,3584]{2,1,0:T(8,128)(2,1)S(1)}, bf16[4,32,3584]{2,1,0:T(8,128)(2,1)S(1)}, u32[]{:S(2)}, u32[]{:S(2)}) collective-permute-start(bf16[4,32,3584]{2,1,0:T(8,128)(2,1)S(1)} %pad_maximum_fusion.10), channel_id=1, source_target_pairs={{0,1},{1,2},{2,3},{3,0},{4,5},{5,6},{6,7},{7,4},{8,9},{9,10},{10,1... | collective-permute-start | bytes 2752520 | tf_op jit(solution)/shard_map/ppermute | solution.py:44
  83.6 11.1 %collective-permute-start.16 = (bf16[4,16,3584]{2,1,0:T(8,128)(2,1)S(1)}, bf16[4,16,3584]{2,1,0:T(8,128)(2,1)S(1)}, u32[]{:S(2)}, u32[]{:S(2)}) collective-permute-start(bf16[4,16,3584]{2,1,0:T(8,128)(2,1)S(1)} %add_convert_fusion.3), channel_id=1, source_target_pairs={{0,12},{1,13},{2,14},{3,15},{4,0},{5,1},{6,2},{7,3},{8,4},{9,5},{1... | collective-permute-start | bytes 1376264 | tf_op jit(solution)/shard_map/ppermute | solution.py:49
  83.8 10.9 %collective-permute-start.17 = (bf16[4,16,3584]{2,1,0:T(8,128)(2,1)S(1)}, bf16[4,16,3584]{2,1,0:T(8,128)(2,1)S(1)}, u32[]{:S(2)}, u32[]{:S(2)}) collective-permute-start(bf16[4,16,3584]{2,1,0:T(8,128)(2,1)S(1)} %add_convert_fusion.2), channel_id=1, source_target_pairs={{0,4},{1,5},{2,6},{3,7},{4,8},{5,9},{6,10},{7,11},{8,12},{9,13},{1... | collective-permute-start | bytes 1376264 | tf_op jit(solution)/shard_map/ppermute | solution.py:48
  87.2 11.5 %collective-permute-start.23 = (bf16[4,16,3584]{2,1,0:T(8,128)(2,1)S(1)}, bf16[4,16,3584]{2,1,0:T(8,128)(2,1)S(1)}, u32[]{:S(2)}, u32[]{:S(2)}) collective-permute-start(bf16[4,16,3584]{2,1,0:T(8,128)(2,1)S(1)} %add_convert_fusion.1), channel_id=1, source_target_pairs={{0,3},{1,0},{2,1},{3,2},{4,7},{5,4},{6,5},{7,6},{8,11},{9,8},{10,9... | collective-permute-start | bytes 1376264 | tf_op jit(solution)/shard_map/ppermute | solution.py:49
  89.8 14.4 %collective-permute-start.24 = (bf16[4,16,3584]{2,1,0:T(8,128)(2,1)S(1)}, bf16[4,16,3584]{2,1,0:T(8,128)(2,1)S(1)}, u32[]{:S(2)}, u32[]{:S(2)}) collective-permute-start(bf16[4,16,3584]{2,1,0:T(8,128)(2,1)S(1)} %add_convert_fusion), channel_id=1, source_target_pairs={{0,1},{1,2},{2,3},{3,0},{4,5},{5,6},{6,7},{7,4},{8,9},{9,10},{10,1... | collective-permute-start | bytes 1376264 | tf_op jit(solution)/shard_map/ppermute | solution.py:48
  95.2 14.2 %collective-permute-start.18 = (bf16[32,3584]{1,0:T(8,128)(2,1)S(1)}, bf16[32,3584]{1,0:T(8,128)(2,1)S(1)}, u32[]{:S(2)}, u32[]{:S(2)}) collective-permute-start(bf16[32,3584]{1,0:T(8,128)(2,1)S(1)} %get-tuple-element.17), channel_id=1, source_target_pairs={{0,1},{1,2},{2,3},{3,0},{4,5},{5,6},{6,7},{7,4},{8,9},{9,10},{10,1... | collective-permute-start | bytes 688136 | tf_op jit(solution)/shard_map/ppermute | solution.py:58
  95.6 14.7 %collective-permute-start.19 = (bf16[32,3584]{1,0:T(8,128)(2,1)S(1)}, bf16[32,3584]{1,0:T(8,128)(2,1)S(1)}, u32[]{:S(2)}, u32[]{:S(2)}) collective-permute-start(bf16[32,3584]{1,0:T(8,128)(2,1)S(1)} %get-tuple-element.19), channel_id=1, source_target_pairs={{0,3},{1,0},{2,1},{3,2},{4,7},{5,4},{6,5},{7,6},{8,11},{9,8},{10,9... | collective-permute-start | bytes 688136 | tf_op jit(solution)/shard_map/ppermute | solution.py:59
  98.5 11.8 %collective-permute-start.20 = (bf16[32,3584]{1,0:T(8,128)(2,1)S(1)}, bf16[32,3584]{1,0:T(8,128)(2,1)S(1)}, u32[]{:S(2)}, u32[]{:S(2)}) collective-permute-start(bf16[32,3584]{1,0:T(8,128)(2,1)S(1)} %get-tuple-element.18), channel_id=1, source_target_pairs={{0,2},{1,3},{2,0},{3,1},{4,6},{5,7},{6,4},{7,5},{8,10},{9,11},{10,... | collective-permute-start | bytes 688136 | tf_op jit(solution)/shard_map/ppermute | solution.py:60
  (8 other events, 48.2 us)

commit v2 on v1

--- a/solution.py
+++ b/solution.py
@@ -87,12 +87,11 @@
     b_y = jnp.stack(_gather_direct(normed[half:], n, "y"))
     a0, a1, a2, a3 = _gather_ring(a_x, n, "y")
     b0, b1, b2, b3 = _gather_ring(b_y, n, "x")
-    near_a = ffn(jnp.stack([a1, a3]))
-    near_b = ffn(jnp.stack([b1, b3]))
+    near = ffn(jnp.stack([a1, a3, b1, b3]))
     far = ffn(jnp.stack([a2, b2]))
     own = ffn(jnp.stack([a0, b0]))
-    out_a = [own[0], near_a[0], far[0], near_a[1]]
-    out_b = [own[1], near_b[0], far[1], near_b[1]]
+    out_a = [own[0], near[0], far[0], near[1]]
+    out_b = [own[1], near[2], far[1], near[3]]
 
     sum_a = _reduce_direct(_reduce_relay(out_a, n, "y"), n, "x")
     sum_b = _reduce_direct(_reduce_relay(out_b, n, "x"), n, "y")

time: 118 us -> 118 us (level)
  waiting for transfers between devices: 50.6 us -> 44.5 us
  starting transfers between devices: 39.9 us -> 45.6 us
    ppermute x2, waiting for transfers between devices: 14.8 us -> 0.01 us  [_reduce_relay(): lax.ppermute(jnp.concatenate([lo(c[2]), hi(c[3])], axis=-2).astype(bf), '...]
    ppermute x2, waiting for transfers between devices: 0.01 us -> 14.6 us  [_reduce_relay(): lax.ppermute(jnp.concatenate([lo(c[1]), hi(c[2])], axis=-2).astype(bf), '...]
    ppermute x2, waiting for transfers between devices: 0.01 us -> 8.01 us  [_gather_ring(): ahead = lax.ppermute(s, 'tensor', _shift(n, axis, -1))]
    ppermute x2, waiting for transfers between devices: 7.08 us -> 0.01 us  [_gather_ring(): behind = lax.ppermute(s, 'tensor', _shift(n, axis, +1))]
    ppermute x2, waiting for transfers between devices: 3.63 us -> 0.21 us  [_gather_direct(): behind = lax.ppermute(s, 'tensor', _shift(n, axis, +1))]
    ppermute x2, starting transfers between devices: 3.13 us -> 0.01 us  [_gather_ring(): behind = lax.ppermute(s, 'tensor', _shift(n, axis, +1))]
    ppermute x2, starting transfers between devices: 3.04 us -> 5.95 us  [_gather_ring(): far_hi = lax.ppermute(ahead[..., h:, :], 'tensor', _shift(n, axis, -1))]
    ppermute x2, waiting for transfers between devices: 5.2 us -> 2.4 us  [_gather_direct(): ahead = lax.ppermute(s, 'tensor', _shift(n, axis, -1))]
  transfers between devices with their start and end apart: 28 -> 28, of which waited for: 14 -> 13; matrix products, arithmetic and copies ran while one was open for 14% -> 15% of each run, Pallas kernels for 0% -> 0%
where the time goes in v2:
time: 118 us
  starting transfers between devices  45.6 us (39%)
  waiting for transfers between devices  44.5 us (38%)
  matrix products  16.3 us (14%)
  other arithmetic  7.3 us (6%)
  local copies, waits for them, and re-layouts  3.4 us (3%)
    ppermute x2, waiting for transfers between devices, _reduce_relay(): lax.ppermute(jnp.concatenate([lo(c[1]), hi(c[2])], axis=-2).astype(bf), '...  14.6 us
    ppermute x2, waiting for transfers between devices, _gather_ring(): ahead = lax.ppermute(s, 'tensor', _shift(n, axis, -1))  8.01 us
    ppermute x2, starting transfers between devices, _gather_ring(): ahead = lax.ppermute(s, 'tensor', _shift(n, axis, -1))  7.78 us
    ppermute x2, waiting for transfers between devices, _reduce_relay(): second_ahead = lax.ppermute(relay_down, 'tensor', down)  6.61 us
    dot_general x3, matrix products, _ffn(): jnp.dot(act, down_weight, preferred_element_type=jnp.float32)  6.51 us
    ppermute x2, starting transfers between devices, _gather_ring(): far_hi = lax.ppermute(ahead[..., h:, :], 'tensor', _shift(n, axis, -1))  5.95 us
    ppermute x2, waiting for transfers between devices, _reduce_relay(): second_behind = lax.ppermute(relay_up, 'tensor', up)  5.22 us
    dot_general x3, matrix products, _ffn(): lax.dot_general(rows, up_weight, dims, preferred_element_type=jnp.float32)  4.95 us
  transfers between devices with their start and end apart: 28, of which 13 were waited for; matrix products, arithmetic and copies ran while one was open for 15% of the time, Pallas kernels for 0%

profile of v2, /device:TPU:24, one launch (start us, length us, event | category | flops | bytes accessed | tf_op | source)
XLA Modules:
  0.0 117.6 jit_solution(619145778534357774)
XLA Ops:
  2.5 2.0 %collective-permute-start.5 = (bf16[32,3584]{1,0:T(8,128)(2,1)S(1)}, bf16[32,3584]{1,0:T(8,128)(2,1)S(1)}, u32[]{:S(2)}, u32[]{:S(2)}) collective-permute-start(bf16[32,3584]{1,0:T(8,128)(2,1)S(1)} %get-tuple-element.33), channel_id=1, source_target_pairs={{0,4},{1,5},{2,6},{3,7},{4,8},{5,9},{6,10},{7,11},{8,12},{9,13},{1... | collective-permute-start | bytes 688136 | tf_op jit(solution)/shard_map/ppermute | solution.py:34
  6.9 2.7 %collective-permute-start.1 = (bf16[32,3584]{1,0:T(8,128)(2,1)S(1)}, bf16[32,3584]{1,0:T(8,128)(2,1)S(1)}, u32[]{:S(2)}, u32[]{:S(2)}) collective-permute-start(bf16[32,3584]{1,0:T(8,128)(2,1)S(1)} %get-tuple-element.34), channel_id=1, source_target_pairs={{0,2},{1,3},{2,0},{3,1},{4,6},{5,7},{6,4},{7,5},{8,10},{9,11},{10,... | collective-permute-start | bytes 688136 | tf_op jit(solution)/shard_map/ppermute | solution.py:35
  11.1 2.8 %collective-permute-start = (bf16[32,3584]{1,0:T(8,128)(2,1)S(1)}, bf16[32,3584]{1,0:T(8,128)(2,1)S(1)}, u32[]{:S(2)}, u32[]{:S(2)}) collective-permute-start(bf16[32,3584]{1,0:T(8,128)(2,1)S(1)} %get-tuple-element.34), channel_id=1, source_target_pairs={{0,3},{1,0},{2,1},{3,2},{4,7},{5,4},{6,5},{7,6},{8,11},{9,8},{10,9... | collective-permute-start | bytes 688136 | tf_op jit(solution)/shard_map/ppermute | solution.py:33
  14.1 2.4 %collective-permute-done.3 = bf16[32,3584]{1,0:T(8,128)(2,1)S(1)} collective-permute-done((bf16[32,3584]{1,0:T(8,128)(2,1)S(1)}, bf16[32,3584]{1,0:T(8,128)(2,1)S(1)}, u32[]{:S(2)}, u32[]{:S(2)}) %collective-permute-start.3) | collective-permute-done | bytes 229408 | tf_op jit(solution)/shard_map/ppermute | solution.py:33
  16.6 2.8 %collective-permute-start.8 = (bf16[4,32,3584]{2,1,0:T(8,128)(2,1)S(1)}, bf16[4,32,3584]{2,1,0:T(8,128)(2,1)S(1)}, u32[]{:S(2)}, u32[]{:S(2)}) collective-permute-start(bf16[4,32,3584]{2,1,0:T(8,128)(2,1)S(1)} %get-tuple-element.29), channel_id=1, source_target_pairs={{0,3},{1,0},{2,1},{3,2},{4,7},{5,4},{6,5},{7,6},{8,11},{9,8},{10,9... | collective-permute-start | bytes 2752520 | tf_op jit(solution)/shard_map/ppermute | solution.py:23
  19.6 4.9 %collective-permute-start.6 = (bf16[4,32,3584]{2,1,0:T(8,128)(2,1)S(1)}, bf16[4,32,3584]{2,1,0:T(8,128)(2,1)S(1)}, u32[]{:S(2)}, u32[]{:S(2)}) collective-permute-start(bf16[4,32,3584]{2,1,0:T(8,128)(2,1)S(1)} %get-tuple-element.27), channel_id=1, source_target_pairs={{0,12},{1,13},{2,14},{3,15},{4,0},{5,1},{6,2},{7,3},{8,4},{9,5},{1... | collective-permute-start | bytes 2752520 | tf_op jit(solution)/shard_map/ppermute | solution.py:23
  29.1 1.6 %convolution_convert_fusion.2 = bf16[256,3584]{1,0:T(8,128)(2,1)S(1)} fusion(bf16[256,576]{0,1:T(8,128)(2,1)S(1)} %fusion.2, bf16[576,3584]{1,0:T(8,128)(2,1)S(1)} %copy-done), kind=kOutput, calls=%fused_computation.2 | convolution fusion | flops 1057882112 | bytes 6258688 | tf_op jit(solution)/shard_map/dot_general | solution.py:70
  31.2 8.0 %collective-permute-done.8 = bf16[4,32,3584]{2,1,0:T(8,128)(2,1)S(1)} collective-permute-done((bf16[4,32,3584]{2,1,0:T(8,128)(2,1)S(1)}, bf16[4,32,3584]{2,1,0:T(8,128)(2,1)S(1)}, u32[]{:S(2)}, u32[]{:S(2)}) %collective-permute-start.8) | collective-permute-done | bytes 917536 | tf_op jit(solution)/shard_map/ppermute | solution.py:23
  39.3 3.8 %collective-permute-start.13 = (bf16[4,16,3584]{2,1,0:T(8,128)(2,1)S(1)}, bf16[4,16,3584]{2,1,0:T(8,128)(2,1)S(1)}, u32[]{:S(2)}, u32[]{:S(2)}) collective-permute-start(bf16[4,16,3584]{2,1,0:T(8,128)(2,1)S(1)} %slice.207), channel_id=1, source_target_pairs={{0,3},{1,0},{2,1},{3,2},{4,7},{5,4},{6,5},{7,6},{8,11},{9,8},{10,9... | collective-permute-start | bytes 1376264 | tf_op jit(solution)/shard_map/ppermute | solution.py:27
  43.4 2.2 %collective-permute-start.11 = (bf16[4,16,3584]{2,1,0:T(8,128)(2,1)S(1)}, bf16[4,16,3584]{2,1,0:T(8,128)(2,1)S(1)}, u32[]{:S(2)}, u32[]{:S(2)}) collective-permute-start(bf16[4,16,3584]{2,1,0:T(8,128)(2,1)S(1)} %slice.205), channel_id=1, source_target_pairs={{0,12},{1,13},{2,14},{3,15},{4,0},{5,1},{6,2},{7,3},{8,4},{9,5},{1... | collective-permute-start | bytes 1376264 | tf_op jit(solution)/shard_map/ppermute | solution.py:27
  47.3 2.3 %fusion.31 = f32[512,576]{0,1:T(8,128)S(1)} fusion(bf16[512,3584]{1,0:T(8,128)(2,1)S(1)} %bitcast.88, bf16[576,3584]{1,0:T(8,128)(2,1)S(1)} %copy-done.1), kind=kOutput, calls=%fused_computation.75 | convolution fusion | flops 2113929216 | bytes 8978432 | tf_op jit(solution)/shard_map/dot_general | solution.py:66
  49.6 2.4 %multiply_convert_fusion = bf16[512,576]{0,1:T(8,128)(2,1)S(1)} fusion(f32[512,576]{0,1:T(8,128)S(1)} %fusion.31, bf16[512,3584]{1,0:T(8,128)(2,1)S(1)} %bitcast.89, bf16[576,3584]{1,0:T(8,128)(2,1)S(1)} %copy-done.2), kind=kOutput, calls=%fused_computation.18 | convolution fusion | flops 2115698688 | bytes 9568256 | tf_op jit(solution)/shard_map/dot_general | solution.py:67
  52.1 3.3 %convolution_convert_fusion = bf16[512,3584]{1,0:T(8,128)(2,1)S(1)} fusion(bf16[512,576]{0,1:T(8,128)(2,1)S(1)} %multiply_convert_fusion, bf16[576,3584]{1,0:T(8,128)(2,1)S(1)} %copy-done), kind=kOutput, calls=%fused_computation | convolution fusion | flops 2115764224 | bytes 8388608 | tf_op jit(solution)/shard_map/dot_general | solution.py:70
  58.8 1.6 %convolution_convert_fusion.1 = bf16[256,3584]{1,0:T(8,128)(2,1)S(1)} fusion(bf16[256,576]{0,1:T(8,128)(2,1)S(1)} %fusion.3, bf16[576,3584]{1,0:T(8,128)(2,1)S(1)} %copy-done), kind=kOutput, calls=%fused_computation.1 | convolution fusion | flops 1057882112 | bytes 6258688 | tf_op jit(solution)/shard_map/dot_general | solution.py:70
  62.1 2.0 %collective-permute-start.22 = (bf16[4,32,3584]{2,1,0:T(8,128)(2,1)S(1)}, bf16[4,32,3584]{2,1,0:T(8,128)(2,1)S(1)}, u32[]{:S(2)}, u32[]{:S(2)}) collective-permute-start(bf16[4,32,3584]{2,1,0:T(8,128)(2,1)S(1)} %pad_maximum_fusion.10), channel_id=1, source_target_pairs={{0,3},{1,0},{2,1},{3,2},{4,7},{5,4},{6,5},{7,6},{8,11},{9,8},{10,9... | collective-permute-start | bytes 2752520 | tf_op jit(solution)/shard_map/ppermute | solution.py:45
  64.3 3.4 %collective-permute-start.14 = (bf16[4,32,3584]{2,1,0:T(8,128)(2,1)S(1)}, bf16[4,32,3584]{2,1,0:T(8,128)(2,1)S(1)}, u32[]{:S(2)}, u32[]{:S(2)}) collective-permute-start(bf16[4,32,3584]{2,1,0:T(8,128)(2,1)S(1)} %pad_maximum_fusion.7), channel_id=1, source_target_pairs={{0,4},{1,5},{2,6},{3,7},{4,8},{5,9},{6,10},{7,11},{8,12},{9,13},{1... | collective-permute-start | bytes 2752520 | tf_op jit(solution)/shard_map/ppermute | solution.py:44
  67.8 14.6 %collective-permute-done.21 = bf16[4,32,3584]{2,1,0:T(8,128)(2,1)S(1)} collective-permute-done((bf16[4,32,3584]{2,1,0:T(8,128)(2,1)S(1)}, bf16[4,32,3584]{2,1,0:T(8,128)(2,1)S(1)}, u32[]{:S(2)}, u32[]{:S(2)}) %collective-permute-start.21) | collective-permute-done | bytes 917536 | tf_op jit(solution)/shard_map/ppermute | solution.py:44
  82.8 3.3 %collective-permute-start.23 = (bf16[4,16,3584]{2,1,0:T(8,128)(2,1)S(1)}, bf16[4,16,3584]{2,1,0:T(8,128)(2,1)S(1)}, u32[]{:S(2)}, u32[]{:S(2)}) collective-permute-start(bf16[4,16,3584]{2,1,0:T(8,128)(2,1)S(1)} %add_convert_fusion.1), channel_id=1, source_target_pairs={{0,3},{1,0},{2,1},{3,2},{4,7},{5,4},{6,5},{7,6},{8,11},{9,8},{10,9... | collective-permute-start | bytes 1376264 | tf_op jit(solution)/shard_map/ppermute | solution.py:49
  86.2 2.6 %collective-permute-start.17 = (bf16[4,16,3584]{2,1,0:T(8,128)(2,1)S(1)}, bf16[4,16,3584]{2,1,0:T(8,128)(2,1)S(1)}, u32[]{:S(2)}, u32[]{:S(2)}) collective-permute-start(bf16[4,16,3584]{2,1,0:T(8,128)(2,1)S(1)} %add_convert_fusion.2), channel_id=1, source_target_pairs={{0,4},{1,5},{2,6},{3,7},{4,8},{5,9},{6,10},{7,11},{8,12},{9,13},{1... | collective-permute-start | bytes 1376264 | tf_op jit(solution)/shard_map/ppermute | solution.py:48
  89.0 4.6 %collective-permute-done.24 = bf16[4,16,3584]{2,1,0:T(8,128)(2,1)S(1)} collective-permute-done((bf16[4,16,3584]{2,1,0:T(8,128)(2,1)S(1)}, bf16[4,16,3584]{2,1,0:T(8,128)(2,1)S(1)}, u32[]{:S(2)}, u32[]{:S(2)}) %collective-permute-start.24) | collective-permute-done | bytes 458784 | tf_op jit(solution)/shard_map/ppermute | solution.py:48
  97.0 1.8 %collective-permute-start.25 = (bf16[32,3584]{1,0:T(8,128)(2,1)S(1)}, bf16[32,3584]{1,0:T(8,128)(2,1)S(1)}, u32[]{:S(2)}, u32[]{:S(2)}) collective-permute-start(bf16[32,3584]{1,0:T(8,128)(2,1)S(1)} %get-tuple-element.22), channel_id=1, source_target_pairs={{0,4},{1,5},{2,6},{3,7},{4,8},{5,9},{6,10},{7,11},{8,12},{9,13},{1... | collective-permute-start | bytes 688136 | tf_op jit(solution)/shard_map/ppermute | solution.py:58
  99.5 6.6 %collective-permute-done.16 = bf16[4,16,3584]{2,1,0:T(8,128)(2,1)S(1)} collective-permute-done((bf16[4,16,3584]{2,1,0:T(8,128)(2,1)S(1)}, bf16[4,16,3584]{2,1,0:T(8,128)(2,1)S(1)}, u32[]{:S(2)}, u32[]{:S(2)}) %collective-permute-start.16) | collective-permute-done | bytes 458784 | tf_op jit(solution)/shard_map/ppermute | solution.py:49
  109.5 4.7 %collective-permute-done.20 = bf16[32,3584]{1,0:T(8,128)(2,1)S(1)} collective-permute-done((bf16[32,3584]{1,0:T(8,128)(2,1)S(1)}, bf16[32,3584]{1,0:T(8,128)(2,1)S(1)}, u32[]{:S(2)}, u32[]{:S(2)}) %collective-permute-start.20) | collective-permute-done | bytes 229408 | tf_op jit(solution)/shard_map/ppermute | solution.py:60
  114.4 2.2 %collective-permute-done.18 = bf16[32,3584]{1,0:T(8,128)(2,1)S(1)} collective-permute-done((bf16[32,3584]{1,0:T(8,128)(2,1)S(1)}, bf16[32,3584]{1,0:T(8,128)(2,1)S(1)}, u32[]{:S(2)}, u32[]{:S(2)}) %collective-permute-start.18) | collective-permute-done | bytes 229408 | tf_op jit(solution)/shard_map/ppermute | solution.py:58
  (94 shorter events, 28.5 us)
Async XLA Ops:
  2.5 8.6 %collective-permute-start.5 = (bf16[32,3584]{1,0:T(8,128)(2,1)S(1)}, bf16[32,3584]{1,0:T(8,128)(2,1)S(1)}, u32[]{:S(2)}, u32[]{:S(2)}) collective-permute-start(bf16[32,3584]{1,0:T(8,128)(2,1)S(1)} %get-tuple-element.33), channel_id=1, source_target_pairs={{0,4},{1,5},{2,6},{3,7},{4,8},{5,9},{6,10},{7,11},{8,12},{9,13},{1... | collective-permute-start | bytes 688136 | tf_op jit(solution)/shard_map/ppermute | solution.py:34
  4.6 9.5 %collective-permute-start.4 = (bf16[32,3584]{1,0:T(8,128)(2,1)S(1)}, bf16[32,3584]{1,0:T(8,128)(2,1)S(1)}, u32[]{:S(2)}, u32[]{:S(2)}) collective-permute-start(bf16[32,3584]{1,0:T(8,128)(2,1)S(1)} %get-tuple-element.33), channel_id=1, source_target_pairs={{0,8},{1,9},{2,10},{3,11},{4,12},{5,13},{6,14},{7,15},{8,0},{9,1},... | collective-permute-start | bytes 688136 | tf_op jit(solution)/shard_map/ppermute | solution.py:35
  5.4 11.1 %collective-permute-start.3 = (bf16[32,3584]{1,0:T(8,128)(2,1)S(1)}, bf16[32,3584]{1,0:T(8,128)(2,1)S(1)}, u32[]{:S(2)}, u32[]{:S(2)}) collective-permute-start(bf16[32,3584]{1,0:T(8,128)(2,1)S(1)} %get-tuple-element.33), channel_id=1, source_target_pairs={{0,12},{1,13},{2,14},{3,15},{4,0},{5,1},{6,2},{7,3},{8,4},{9,5},{1... | collective-permute-start | bytes 688136 | tf_op jit(solution)/shard_map/ppermute | solution.py:33
  5.5 13.9 %collective-permute-start.2 = (bf16[32,3584]{1,0:T(8,128)(2,1)S(1)}, bf16[32,3584]{1,0:T(8,128)(2,1)S(1)}, u32[]{:S(2)}, u32[]{:S(2)}) collective-permute-start(bf16[32,3584]{1,0:T(8,128)(2,1)S(1)} %get-tuple-element.34), channel_id=1, source_target_pairs={{0,1},{1,2},{2,3},{3,0},{4,5},{5,6},{6,7},{7,4},{8,9},{9,10},{10,1... | collective-permute-start | bytes 688136 | tf_op jit(solution)/shard_map/ppermute | solution.py:34
  6.9 12.6 %collective-permute-start.1 = (bf16[32,3584]{1,0:T(8,128)(2,1)S(1)}, bf16[32,3584]{1,0:T(8,128)(2,1)S(1)}, u32[]{:S(2)}, u32[]{:S(2)}) collective-permute-start(bf16[32,3584]{1,0:T(8,128)(2,1)S(1)} %get-tuple-element.34), channel_id=1, source_target_pairs={{0,2},{1,3},{2,0},{3,1},{4,6},{5,7},{6,4},{7,5},{8,10},{9,11},{10,... | collective-permute-start | bytes 688136 | tf_op jit(solution)/shard_map/ppermute | solution.py:35
  16.6 22.6 %collective-permute-start.8 = (bf16[4,32,3584]{2,1,0:T(8,128)(2,1)S(1)}, bf16[4,32,3584]{2,1,0:T(8,128)(2,1)S(1)}, u32[]{:S(2)}, u32[]{:S(2)}) collective-permute-start(bf16[4,32,3584]{2,1,0:T(8,128)(2,1)S(1)} %get-tuple-element.29), channel_id=1, source_target_pairs={{0,3},{1,0},{2,1},{3,2},{4,7},{5,4},{6,5},{7,6},{8,11},{9,8},{10,9... | collective-permute-start | bytes 2752520 | tf_op jit(solution)/shard_map/ppermute | solution.py:23
  19.4 23.6 %collective-permute-start.9 = (bf16[4,32,3584]{2,1,0:T(8,128)(2,1)S(1)}, bf16[4,32,3584]{2,1,0:T(8,128)(2,1)S(1)}, u32[]{:S(2)}, u32[]{:S(2)}) collective-permute-start(bf16[4,32,3584]{2,1,0:T(8,128)(2,1)S(1)} %get-tuple-element.29), channel_id=1, source_target_pairs={{0,1},{1,2},{2,3},{3,0},{4,5},{5,6},{6,7},{7,4},{8,9},{9,10},{10,1... | collective-permute-start | bytes 2752520 | tf_op jit(solution)/shard_map/ppermute | solution.py:24
  19.6 23.7 %collective-permute-start.6 = (bf16[4,32,3584]{2,1,0:T(8,128)(2,1)S(1)}, bf16[4,32,3584]{2,1,0:T(8,128)(2,1)S(1)}, u32[]{:S(2)}, u32[]{:S(2)}) collective-permute-start(bf16[4,32,3584]{2,1,0:T(8,128)(2,1)S(1)} %get-tuple-element.27), channel_id=1, source_target_pairs={{0,12},{1,13},{2,14},{3,15},{4,0},{5,1},{6,2},{7,3},{8,4},{9,5},{1... | collective-permute-start | bytes 2752520 | tf_op jit(solution)/shard_map/ppermute | solution.py:23
  24.6 21.0 %collective-permute-start.7 = (bf16[4,32,3584]{2,1,0:T(8,128)(2,1)S(1)}, bf16[4,32,3584]{2,1,0:T(8,128)(2,1)S(1)}, u32[]{:S(2)}, u32[]{:S(2)}) collective-permute-start(bf16[4,32,3584]{2,1,0:T(8,128)(2,1)S(1)} %get-tuple-element.27), channel_id=1, source_target_pairs={{0,4},{1,5},{2,6},{3,7},{4,8},{5,9},{6,10},{7,11},{8,12},{9,13},{1... | collective-permute-start | bytes 2752520 | tf_op jit(solution)/shard_map/ppermute | solution.py:24
  39.3 16.5 %collective-permute-start.13 = (bf16[4,16,3584]{2,1,0:T(8,128)(2,1)S(1)}, bf16[4,16,3584]{2,1,0:T(8,128)(2,1)S(1)}, u32[]{:S(2)}, u32[]{:S(2)}) collective-permute-start(bf16[4,16,3584]{2,1,0:T(8,128)(2,1)S(1)} %slice.207), channel_id=1, source_target_pairs={{0,3},{1,0},{2,1},{3,2},{4,7},{5,4},{6,5},{7,6},{8,11},{9,8},{10,9... | collective-permute-start | bytes 1376264 | tf_op jit(solution)/shard_map/ppermute | solution.py:27
  43.1 12.8 %collective-permute-start.12 = (bf16[4,16,3584]{2,1,0:T(8,128)(2,1)S(1)}, bf16[4,16,3584]{2,1,0:T(8,128)(2,1)S(1)}, u32[]{:S(2)}, u32[]{:S(2)}) collective-permute-start(bf16[4,16,3584]{2,1,0:T(8,128)(2,1)S(1)} %slice.206), channel_id=1, source_target_pairs={{0,1},{1,2},{2,3},{3,0},{4,5},{5,6},{6,7},{7,4},{8,9},{9,10},{10,1... | collective-permute-start | bytes 1376264 | tf_op jit(solution)/shard_map/ppermute | solution.py:26
  43.4 12.6 %collective-permute-start.11 = (bf16[4,16,3584]{2,1,0:T(8,128)(2,1)S(1)}, bf16[4,16,3584]{2,1,0:T(8,128)(2,1)S(1)}, u32[]{:S(2)}, u32[]{:S(2)}) collective-permute-start(bf16[4,16,3584]{2,1,0:T(8,128)(2,1)S(1)} %slice.205), channel_id=1, source_target_pairs={{0,12},{1,13},{2,14},{3,15},{4,0},{5,1},{6,2},{7,3},{8,4},{9,5},{1... | collective-permute-start | bytes 1376264 | tf_op jit(solution)/shard_map/ppermute | solution.py:27
  45.6 10.4 %collective-permute-start.10 = (bf16[4,16,3584]{2,1,0:T(8,128)(2,1)S(1)}, bf16[4,16,3584]{2,1,0:T(8,128)(2,1)S(1)}, u32[]{:S(2)}, u32[]{:S(2)}) collective-permute-start(bf16[4,16,3584]{2,1,0:T(8,128)(2,1)S(1)} %slice.204), channel_id=1, source_target_pairs={{0,4},{1,5},{2,6},{3,7},{4,8},{5,9},{6,10},{7,11},{8,12},{9,13},{1... | collective-permute-start | bytes 1376264 | tf_op jit(solution)/shard_map/ppermute | solution.py:26
  60.7 21.7 %collective-permute-start.21 = (bf16[4,32,3584]{2,1,0:T(8,128)(2,1)S(1)}, bf16[4,32,3584]{2,1,0:T(8,128)(2,1)S(1)}, u32[]{:S(2)}, u32[]{:S(2)}) collective-permute-start(bf16[4,32,3584]{2,1,0:T(8,128)(2,1)S(1)} %pad_maximum_fusion.9), channel_id=1, source_target_pairs={{0,1},{1,2},{2,3},{3,0},{4,5},{5,6},{6,7},{7,4},{8,9},{9,10},{10,1... | collective-permute-start | bytes 2752520 | tf_op jit(solution)/shard_map/ppermute | solution.py:44
  62.1 20.5 %collective-permute-start.22 = (bf16[4,32,3584]{2,1,0:T(8,128)(2,1)S(1)}, bf16[4,32,3584]{2,1,0:T(8,128)(2,1)S(1)}, u32[]{:S(2)}, u32[]{:S(2)}) collective-permute-start(bf16[4,32,3584]{2,1,0:T(8,128)(2,1)S(1)} %pad_maximum_fusion.10), channel_id=1, source_target_pairs={{0,3},{1,0},{2,1},{3,2},{4,7},{5,4},{6,5},{7,6},{8,11},{9,8},{10,9... | collective-permute-start | bytes 2752520 | tf_op jit(solution)/shard_map/ppermute | solution.py:45
  64.3 21.8 %collective-permute-start.14 = (bf16[4,32,3584]{2,1,0:T(8,128)(2,1)S(1)}, bf16[4,32,3584]{2,1,0:T(8,128)(2,1)S(1)}, u32[]{:S(2)}, u32[]{:S(2)}) collective-permute-start(bf16[4,32,3584]{2,1,0:T(8,128)(2,1)S(1)} %pad_maximum_fusion.7), channel_id=1, source_target_pairs={{0,4},{1,5},{2,6},{3,7},{4,8},{5,9},{6,10},{7,11},{8,12},{9,13},{1... | collective-permute-start | bytes 2752520 | tf_op jit(solution)/shard_map/ppermute | solution.py:44
  67.7 21.1 %collective-permute-start.15 = (bf16[4,32,3584]{2,1,0:T(8,128)(2,1)S(1)}, bf16[4,32,3584]{2,1,0:T(8,128)(2,1)S(1)}, u32[]{:S(2)}, u32[]{:S(2)}) collective-permute-start(bf16[4,32,3584]{2,1,0:T(8,128)(2,1)S(1)} %pad_maximum_fusion.8), channel_id=1, source_target_pairs={{0,12},{1,13},{2,14},{3,15},{4,0},{5,1},{6,2},{7,3},{8,4},{9,5},{1... | collective-permute-start | bytes 2752520 | tf_op jit(solution)/shard_map/ppermute | solution.py:45
  82.6 11.0 %collective-permute-start.24 = (bf16[4,16,3584]{2,1,0:T(8,128)(2,1)S(1)}, bf16[4,16,3584]{2,1,0:T(8,128)(2,1)S(1)}, u32[]{:S(2)}, u32[]{:S(2)}) collective-permute-start(bf16[4,16,3584]{2,1,0:T(8,128)(2,1)S(1)} %add_convert_fusion), channel_id=1, source_target_pairs={{0,1},{1,2},{2,3},{3,0},{4,5},{5,6},{6,7},{7,4},{8,9},{9,10},{10,1... | collective-permute-start | bytes 1376264 | tf_op jit(solution)/shard_map/ppermute | solution.py:48
  82.8 10.8 %collective-permute-start.23 = (bf16[4,16,3584]{2,1,0:T(8,128)(2,1)S(1)}, bf16[4,16,3584]{2,1,0:T(8,128)(2,1)S(1)}, u32[]{:S(2)}, u32[]{:S(2)}) collective-permute-start(bf16[4,16,3584]{2,1,0:T(8,128)(2,1)S(1)} %add_convert_fusion.1), channel_id=1, source_target_pairs={{0,3},{1,0},{2,1},{3,2},{4,7},{5,4},{6,5},{7,6},{8,11},{9,8},{10,9... | collective-permute-start | bytes 1376264 | tf_op jit(solution)/shard_map/ppermute | solution.py:49
  86.2 13.3 %collective-permute-start.17 = (bf16[4,16,3584]{2,1,0:T(8,128)(2,1)S(1)}, bf16[4,16,3584]{2,1,0:T(8,128)(2,1)S(1)}, u32[]{:S(2)}, u32[]{:S(2)}) collective-permute-start(bf16[4,16,3584]{2,1,0:T(8,128)(2,1)S(1)} %add_convert_fusion.2), channel_id=1, source_target_pairs={{0,4},{1,5},{2,6},{3,7},{4,8},{5,9},{6,10},{7,11},{8,12},{9,13},{1... | collective-permute-start | bytes 1376264 | tf_op jit(solution)/shard_map/ppermute | solution.py:48
  88.9 17.1 %collective-permute-start.16 = (bf16[4,16,3584]{2,1,0:T(8,128)(2,1)S(1)}, bf16[4,16,3584]{2,1,0:T(8,128)(2,1)S(1)}, u32[]{:S(2)}, u32[]{:S(2)}) collective-permute-start(bf16[4,16,3584]{2,1,0:T(8,128)(2,1)S(1)} %add_convert_fusion.3), channel_id=1, source_target_pairs={{0,12},{1,13},{2,14},{3,15},{4,0},{5,1},{6,2},{7,3},{8,4},{9,5},{1... | collective-permute-start | bytes 1376264 | tf_op jit(solution)/shard_map/ppermute | solution.py:49
  94.0 14.2 %collective-permute-start.27 = (bf16[32,3584]{1,0:T(8,128)(2,1)S(1)}, bf16[32,3584]{1,0:T(8,128)(2,1)S(1)}, u32[]{:S(2)}, u32[]{:S(2)}) collective-permute-start(bf16[32,3584]{1,0:T(8,128)(2,1)S(1)} %get-tuple-element.23), channel_id=1, source_target_pairs={{0,8},{1,9},{2,10},{3,11},{4,12},{5,13},{6,14},{7,15},{8,0},{9,1},... | collective-permute-start | bytes 688136 | tf_op jit(solution)/shard_map/ppermute | solution.py:60
  95.5 13.9 %collective-permute-start.26 = (bf16[32,3584]{1,0:T(8,128)(2,1)S(1)}, bf16[32,3584]{1,0:T(8,128)(2,1)S(1)}, u32[]{:S(2)}, u32[]{:S(2)}) collective-permute-start(bf16[32,3584]{1,0:T(8,128)(2,1)S(1)} %get-tuple-element.24), channel_id=1, source_target_pairs={{0,12},{1,13},{2,14},{3,15},{4,0},{5,1},{6,2},{7,3},{8,4},{9,5},{1... | collective-permute-start | bytes 688136 | tf_op jit(solution)/shard_map/ppermute | solution.py:59
  97.0 12.4 %collective-permute-start.25 = (bf16[32,3584]{1,0:T(8,128)(2,1)S(1)}, bf16[32,3584]{1,0:T(8,128)(2,1)S(1)}, u32[]{:S(2)}, u32[]{:S(2)}) collective-permute-start(bf16[32,3584]{1,0:T(8,128)(2,1)S(1)} %get-tuple-element.22), channel_id=1, source_target_pairs={{0,4},{1,5},{2,6},{3,7},{4,8},{5,9},{6,10},{7,11},{8,12},{9,13},{1... | collective-permute-start | bytes 688136 | tf_op jit(solution)/shard_map/ppermute | solution.py:58
  (8 other events, 50.7 us)

commit v3 on v2

--- a/solution.py
+++ b/solution.py
@@ -36,20 +36,28 @@
     return [s, ahead, far, behind]
 
 
-def _reduce_relay(c, n, axis):
+def _reduce_relay(c, n, axis, split_far=False):
     h = c[0].shape[-2] // 2
     lo, hi = (lambda v: v[..., :h, :]), (lambda v: v[..., h:, :])
     bf, f32 = jnp.bfloat16, jnp.float32
     up, down = _shift(n, axis, +1), _shift(n, axis, -1)
-    from_behind = lax.ppermute(jnp.concatenate([lo(c[1]), hi(c[2])], axis=-2).astype(bf), "tensor", up)
-    from_ahead = lax.ppermute(jnp.concatenate([lo(c[2]), hi(c[3])], axis=-2).astype(bf), "tensor", down)
-    relay_up = (hi(c[1]).astype(f32) + hi(from_behind).astype(f32)).astype(bf)
-    relay_down = (lo(c[3]).astype(f32) + lo(from_ahead).astype(f32)).astype(bf)
+    if split_far:
+        far_behind = lax.ppermute(hi(c[2]).astype(bf), "tensor", up)
+        far_ahead = lax.ppermute(lo(c[2]).astype(bf), "tensor", down)
+        near_behind = lax.ppermute(lo(c[1]).astype(bf), "tensor", up)
+        near_ahead = lax.ppermute(hi(c[3]).astype(bf), "tensor", down)
+    else:
+        from_behind = lax.ppermute(jnp.concatenate([lo(c[1]), hi(c[2])], axis=-2).astype(bf), "tensor", up)
+        from_ahead = lax.ppermute(jnp.concatenate([lo(c[2]), hi(c[3])], axis=-2).astype(bf), "tensor", down)
+        near_behind, far_behind = lo(from_behind), hi(from_behind)
+        far_ahead, near_ahead = lo(from_ahead), hi(from_ahead)
+    relay_up = (hi(c[1]).astype(f32) + far_behind.astype(f32)).astype(bf)
+    relay_down = (lo(c[3]).astype(f32) + far_ahead.astype(f32)).astype(bf)
     second_behind = lax.ppermute(relay_up, "tensor", up)
     second_ahead = lax.ppermute(relay_down, "tensor", down)
     own = c[0].astype(f32)
-    sum_lo = lo(own) + lo(from_behind).astype(f32) + second_ahead.astype(f32)
-    sum_hi = hi(own) + hi(from_ahead).astype(f32) + second_behind.astype(f32)
+    sum_lo = lo(own) + near_behind.astype(f32) + second_ahead.astype(f32)
+    sum_hi = hi(own) + near_ahead.astype(f32) + second_behind.astype(f32)
     return jnp.concatenate([sum_lo, sum_hi], axis=-2)
 
 
@@ -94,7 +102,7 @@
     out_b = [own[1], near[2], far[1], near[3]]
 
     sum_a = _reduce_direct(_reduce_relay(out_a, n, "y"), n, "x")
-    sum_b = _reduce_direct(_reduce_relay(out_b, n, "x"), n, "y")
+    sum_b = _reduce_direct(_reduce_relay(out_b, n, "x", split_far=True), n, "y")
     result = jnp.concatenate([sum_a, sum_b], axis=0).astype(jnp.bfloat16)
     live_mask = jnp.arange(capacity, dtype=jnp.int32) < span_lengths[own_rank]
     return jnp.where(live_mask[:, None], result, jnp.zeros_like(result))

time: 118 us -> 130 us (1.10)
  waiting for transfers between devices: 44.5 us -> 60.6 us
  starting transfers between devices: 45.6 us -> 41.5 us
    ppermute x0 -> x4, waiting for transfers between devices: none -> 12.6 us  [the longest x1 12.6 us: _reduce_relay(): far_behind = lax.ppermute(hi(c[2]).astype(bf), 'tensor', up)]
    ppermute x2 -> x1, waiting for transfers between devices: 0.01 us -> 12 us  [_reduce_relay(): lax.ppermute(jnp.concatenate([lo(c[2]), hi(c[3])], axis=-2).astype(bf), '...]
    ppermute x2 -> x1, waiting for transfers between devices: 14.6 us -> 6.43 us  [_reduce_relay(): lax.ppermute(jnp.concatenate([lo(c[1]), hi(c[2])], axis=-2).astype(bf), '...]
    ppermute x0 -> x4, starting transfers between devices: none -> 6.99 us  [the longest x1 3.29 us: _reduce_relay(): near_ahead = lax.ppermute(hi(c[3]).astype(bf), 'tensor', down)]
    ppermute x2 -> x1, starting transfers between devices: 4.74 us -> 0.12 us  [_reduce_relay(): lax.ppermute(jnp.concatenate([lo(c[1]), hi(c[2])], axis=-2).astype(bf), '...]
    ppermute x2, waiting for transfers between devices: 6.61 us -> 3.94 us  [_reduce_relay(): second_ahead = lax.ppermute(relay_down, 'tensor', down)]
    ppermute x2, starting transfers between devices: 2.7 us -> 0.09 us  [_reduce_relay(): second_behind = lax.ppermute(relay_up, 'tensor', up)]
    ppermute x2, starting transfers between devices: 2.39 us -> 0.19 us  [_reduce_direct(): from_far = lax.ppermute(c[2].astype(bf), 'tensor', _shift(n, axis, +2))]
  transfers between devices with their start and end apart: 28 -> 30, of which waited for: 13 -> 12; matrix products, arithmetic and copies ran while one was open for 15% -> 17% of each run, Pallas kernels for 0% -> 0%
where the time goes in v3:
time: 130 us; the launch traced here: 129 us
  waiting for transfers between devices  60.6 us (47%)
  starting transfers between devices  41.5 us (32%)
  matrix products  16.3 us (13%)
  other arithmetic  7.08 us (5%)
  local copies, waits for them, and re-layouts  3.4 us (3%)
    ppermute x1, waiting for transfers between devices, _reduce_relay(): far_behind = lax.ppermute(hi(c[2]).astype(bf), 'tensor', up)  12.6 us
    ppermute x1, waiting for transfers between devices, _reduce_relay(): lax.ppermute(jnp.concatenate([lo(c[2]), hi(c[3])], axis=-2).astype(bf), '...  12 us
    ppermute x2, waiting for transfers between devices, _gather_ring(): ahead = lax.ppermute(s, 'tensor', _shift(n, axis, -1))  8.01 us
    ppermute x2, starting transfers between devices, _gather_ring(): ahead = lax.ppermute(s, 'tensor', _shift(n, axis, -1))  7.78 us
    ppermute x2, waiting for transfers between devices, _reduce_relay(): second_behind = lax.ppermute(relay_up, 'tensor', up)  7.19 us
    dot_general x3, matrix products, _ffn(): jnp.dot(act, down_weight, preferred_element_type=jnp.float32)  6.51 us
    ppermute x1, waiting for transfers between devices, _reduce_relay(): lax.ppermute(jnp.concatenate([lo(c[1]), hi(c[2])], axis=-2).astype(bf), '...  6.43 us
    ppermute x2, starting transfers between devices, _gather_ring(): far_hi = lax.ppermute(ahead[..., h:, :], 'tensor', _shift(n, axis, -1))  5.95 us
  transfers between devices with their start and end apart: 30, of which 12 were waited for; matrix products, arithmetic and copies ran while one was open for 17% of the time, Pallas kernels for 0%

profile of v3, /device:TPU:24, one launch (start us, length us, event | category | flops | bytes accessed | tf_op | source)
XLA Modules:
  0.0 129.4 jit_solution(5645442293908503816)
XLA Ops:
  2.5 2.0 %collective-permute-start.5 = (bf16[32,3584]{1,0:T(8,128)(2,1)S(1)}, bf16[32,3584]{1,0:T(8,128)(2,1)S(1)}, u32[]{:S(2)}, u32[]{:S(2)}) collective-permute-start(bf16[32,3584]{1,0:T(8,128)(2,1)S(1)} %get-tuple-element.33), channel_id=1, source_target_pairs={{0,4},{1,5},{2,6},{3,7},{4,8},{5,9},{6,10},{7,11},{8,12},{9,13},{1... | collective-permute-start | bytes 688136 | tf_op jit(solution)/shard_map/ppermute | solution.py:34
  6.9 2.7 %collective-permute-start.1 = (bf16[32,3584]{1,0:T(8,128)(2,1)S(1)}, bf16[32,3584]{1,0:T(8,128)(2,1)S(1)}, u32[]{:S(2)}, u32[]{:S(2)}) collective-permute-start(bf16[32,3584]{1,0:T(8,128)(2,1)S(1)} %get-tuple-element.34), channel_id=1, source_target_pairs={{0,2},{1,3},{2,0},{3,1},{4,6},{5,7},{6,4},{7,5},{8,10},{9,11},{10,... | collective-permute-start | bytes 688136 | tf_op jit(solution)/shard_map/ppermute | solution.py:35
  11.1 2.8 %collective-permute-start = (bf16[32,3584]{1,0:T(8,128)(2,1)S(1)}, bf16[32,3584]{1,0:T(8,128)(2,1)S(1)}, u32[]{:S(2)}, u32[]{:S(2)}) collective-permute-start(bf16[32,3584]{1,0:T(8,128)(2,1)S(1)} %get-tuple-element.34), channel_id=1, source_target_pairs={{0,3},{1,0},{2,1},{3,2},{4,7},{5,4},{6,5},{7,6},{8,11},{9,8},{10,9... | collective-permute-start | bytes 688136 | tf_op jit(solution)/shard_map/ppermute | solution.py:33
  14.1 2.4 %collective-permute-done.3 = bf16[32,3584]{1,0:T(8,128)(2,1)S(1)} collective-permute-done((bf16[32,3584]{1,0:T(8,128)(2,1)S(1)}, bf16[32,3584]{1,0:T(8,128)(2,1)S(1)}, u32[]{:S(2)}, u32[]{:S(2)}) %collective-permute-start.3) | collective-permute-done | bytes 229408 | tf_op jit(solution)/shard_map/ppermute | solution.py:33
  16.6 2.8 %collective-permute-start.8 = (bf16[4,32,3584]{2,1,0:T(8,128)(2,1)S(1)}, bf16[4,32,3584]{2,1,0:T(8,128)(2,1)S(1)}, u32[]{:S(2)}, u32[]{:S(2)}) collective-permute-start(bf16[4,32,3584]{2,1,0:T(8,128)(2,1)S(1)} %get-tuple-element.29), channel_id=1, source_target_pairs={{0,3},{1,0},{2,1},{3,2},{4,7},{5,4},{6,5},{7,6},{8,11},{9,8},{10,9... | collective-permute-start | bytes 2752520 | tf_op jit(solution)/shard_map/ppermute | solution.py:23
  19.6 4.9 %collective-permute-start.6 = (bf16[4,32,3584]{2,1,0:T(8,128)(2,1)S(1)}, bf16[4,32,3584]{2,1,0:T(8,128)(2,1)S(1)}, u32[]{:S(2)}, u32[]{:S(2)}) collective-permute-start(bf16[4,32,3584]{2,1,0:T(8,128)(2,1)S(1)} %get-tuple-element.27), channel_id=1, source_target_pairs={{0,12},{1,13},{2,14},{3,15},{4,0},{5,1},{6,2},{7,3},{8,4},{9,5},{1... | collective-permute-start | bytes 2752520 | tf_op jit(solution)/shard_map/ppermute | solution.py:23
  31.2 8.0 %collective-permute-done.8 = bf16[4,32,3584]{2,1,0:T(8,128)(2,1)S(1)} collective-permute-done((bf16[4,32,3584]{2,1,0:T(8,128)(2,1)S(1)}, bf16[4,32,3584]{2,1,0:T(8,128)(2,1)S(1)}, u32[]{:S(2)}, u32[]{:S(2)}) %collective-permute-start.8) | collective-permute-done | bytes 917536 | tf_op jit(solution)/shard_map/ppermute | solution.py:23
  39.3 3.8 %collective-permute-start.13 = (bf16[4,16,3584]{2,1,0:T(8,128)(2,1)S(1)}, bf16[4,16,3584]{2,1,0:T(8,128)(2,1)S(1)}, u32[]{:S(2)}, u32[]{:S(2)}) collective-permute-start(bf16[4,16,3584]{2,1,0:T(8,128)(2,1)S(1)} %slice.191), channel_id=1, source_target_pairs={{0,3},{1,0},{2,1},{3,2},{4,7},{5,4},{6,5},{7,6},{8,11},{9,8},{10,9... | collective-permute-start | bytes 1376264 | tf_op jit(solution)/shard_map/ppermute | solution.py:27
  43.4 2.2 %collective-permute-start.11 = (bf16[4,16,3584]{2,1,0:T(8,128)(2,1)S(1)}, bf16[4,16,3584]{2,1,0:T(8,128)(2,1)S(1)}, u32[]{:S(2)}, u32[]{:S(2)}) collective-permute-start(bf16[4,16,3584]{2,1,0:T(8,128)(2,1)S(1)} %slice.189), channel_id=1, source_target_pairs={{0,12},{1,13},{2,14},{3,15},{4,0},{5,1},{6,2},{7,3},{8,4},{9,5},{1... | collective-permute-start | bytes 1376264 | tf_op jit(solution)/shard_map/ppermute | solution.py:27
  47.3 2.3 %fusion.31 = f32[512,576]{0,1:T(8,128)S(1)} fusion(bf16[512,3584]{1,0:T(8,128)(2,1)S(1)} %bitcast.88, bf16[576,3584]{1,0:T(8,128)(2,1)S(1)} %copy-done.1), kind=kOutput, calls=%fused_computation.73 | convolution fusion | flops 2113929216 | bytes 8978432 | tf_op jit(solution)/shard_map/dot_general | solution.py:74
  49.6 2.4 %multiply_convert_fusion = bf16[512,576]{0,1:T(8,128)(2,1)S(1)} fusion(f32[512,576]{0,1:T(8,128)S(1)} %fusion.31, bf16[512,3584]{1,0:T(8,128)(2,1)S(1)} %bitcast.89, bf16[576,3584]{1,0:T(8,128)(2,1)S(1)} %copy-done.2), kind=kOutput, calls=%fused_computation.18 | convolution fusion | flops 2115698688 | bytes 9568256 | tf_op jit(solution)/shard_map/dot_general | solution.py:75
  52.1 3.3 %convolution_convert_fusion = bf16[512,3584]{1,0:T(8,128)(2,1)S(1)} fusion(bf16[512,576]{0,1:T(8,128)(2,1)S(1)} %multiply_convert_fusion, bf16[576,3584]{1,0:T(8,128)(2,1)S(1)} %copy-done), kind=kOutput, calls=%fused_computation | convolution fusion | flops 2115764224 | bytes 8388608 | tf_op jit(solution)/shard_map/dot_general | solution.py:78
  55.7 3.3 %collective-permute-start.24 = (bf16[4,16,3584]{2,1,0:T(8,128)(2,1)S(1)}, bf16[4,16,3584]{2,1,0:T(8,128)(2,1)S(1)}, u32[]{:S(2)}, u32[]{:S(2)}) collective-permute-start(bf16[4,16,3584]{2,1,0:T(8,128)(2,1)S(1)} %slice.218), channel_id=1, source_target_pairs={{0,3},{1,0},{2,1},{3,2},{4,7},{5,4},{6,5},{7,6},{8,11},{9,8},{10,9... | collective-permute-start | bytes 1376264 | tf_op jit(solution)/shard_map/ppermute | solution.py:48
  64.2 3.3 %collective-permute-start.22 = (bf16[4,16,3584]{2,1,0:T(8,128)(2,1)S(1)}, bf16[4,16,3584]{2,1,0:T(8,128)(2,1)S(1)}, u32[]{:S(2)}, u32[]{:S(2)}) collective-permute-start(bf16[4,16,3584]{2,1,0:T(8,128)(2,1)S(1)} %get-tuple-element.26), channel_id=1, source_target_pairs={{0,3},{1,0},{2,1},{3,2},{4,7},{5,4},{6,5},{7,6},{8,11},{9,8},{10,9... | collective-permute-start | bytes 1376264 | tf_op jit(solution)/shard_map/ppermute | solution.py:46
  67.8 12.6 %collective-permute-done.25 = bf16[4,16,3584]{2,1,0:T(8,128)(2,1)S(1)} collective-permute-done((bf16[4,16,3584]{2,1,0:T(8,128)(2,1)S(1)}, bf16[4,16,3584]{2,1,0:T(8,128)(2,1)S(1)}, u32[]{:S(2)}, u32[]{:S(2)}) %collective-permute-start.25) | collective-permute-done | bytes 458784 | tf_op jit(solution)/shard_map/ppermute | solution.py:45
  80.7 6.4 %collective-permute-done.14 = bf16[4,32,3584]{2,1,0:T(8,128)(2,1)S(1)} collective-permute-done((bf16[4,32,3584]{2,1,0:T(8,128)(2,1)S(1)}, bf16[4,32,3584]{2,1,0:T(8,128)(2,1)S(1)}, u32[]{:S(2)}, u32[]{:S(2)}) %collective-permute-start.14) | collective-permute-done | bytes 917536 | tf_op jit(solution)/shard_map/ppermute | solution.py:50
  88.7 12.0 %collective-permute-done.15 = bf16[4,32,3584]{2,1,0:T(8,128)(2,1)S(1)} collective-permute-done((bf16[4,32,3584]{2,1,0:T(8,128)(2,1)S(1)}, bf16[4,32,3584]{2,1,0:T(8,128)(2,1)S(1)}, u32[]{:S(2)}, u32[]{:S(2)}) %collective-permute-start.15) | collective-permute-done | bytes 917536 | tf_op jit(solution)/shard_map/ppermute | solution.py:51
  100.8 2.1 %collective-permute-start.16 = (bf16[4,16,3584]{2,1,0:T(8,128)(2,1)S(1)}, bf16[4,16,3584]{2,1,0:T(8,128)(2,1)S(1)}, u32[]{:S(2)}, u32[]{:S(2)}) collective-permute-start(bf16[4,16,3584]{2,1,0:T(8,128)(2,1)S(1)} %add_convert_fusion.3), channel_id=1, source_target_pairs={{0,12},{1,13},{2,14},{3,15},{4,0},{5,1},{6,2},{7,3},{8,4},{9,5},{1... | collective-permute-start | bytes 1376264 | tf_op jit(solution)/shard_map/ppermute | solution.py:57
  103.5 2.1 %collective-permute-start.28 = (bf16[32,3584]{1,0:T(8,128)(2,1)S(1)}, bf16[32,3584]{1,0:T(8,128)(2,1)S(1)}, u32[]{:S(2)}, u32[]{:S(2)}) collective-permute-start(bf16[32,3584]{1,0:T(8,128)(2,1)S(1)} %get-tuple-element.24), channel_id=1, source_target_pairs={{0,12},{1,13},{2,14},{3,15},{4,0},{5,1},{6,2},{7,3},{8,4},{9,5},{1... | collective-permute-start | bytes 688136 | tf_op jit(solution)/shard_map/ppermute | solution.py:67
  106.8 7.2 %collective-permute-done.17 = bf16[4,16,3584]{2,1,0:T(8,128)(2,1)S(1)} collective-permute-done((bf16[4,16,3584]{2,1,0:T(8,128)(2,1)S(1)}, bf16[4,16,3584]{2,1,0:T(8,128)(2,1)S(1)}, u32[]{:S(2)}, u32[]{:S(2)}) %collective-permute-start.17) | collective-permute-done | bytes 458784 | tf_op jit(solution)/shard_map/ppermute | solution.py:56
  114.0 3.9 %collective-permute-done.16 = bf16[4,16,3584]{2,1,0:T(8,128)(2,1)S(1)} collective-permute-done((bf16[4,16,3584]{2,1,0:T(8,128)(2,1)S(1)}, bf16[4,16,3584]{2,1,0:T(8,128)(2,1)S(1)}, u32[]{:S(2)}, u32[]{:S(2)}) %collective-permute-start.16) | collective-permute-done | bytes 458784 | tf_op jit(solution)/shard_map/ppermute | solution.py:57
  118.4 2.2 %collective-permute-start.19 = (bf16[32,3584]{1,0:T(8,128)(2,1)S(1)}, bf16[32,3584]{1,0:T(8,128)(2,1)S(1)}, u32[]{:S(2)}, u32[]{:S(2)}) collective-permute-start(bf16[32,3584]{1,0:T(8,128)(2,1)S(1)} %get-tuple-element.19), channel_id=1, source_target_pairs={{0,3},{1,0},{2,1},{3,2},{4,7},{5,4},{6,5},{7,6},{8,11},{9,8},{10,9... | collective-permute-start | bytes 688136 | tf_op jit(solution)/shard_map/ppermute | solution.py:67
  120.8 5.2 %collective-permute-done.20 = bf16[32,3584]{1,0:T(8,128)(2,1)S(1)} collective-permute-done((bf16[32,3584]{1,0:T(8,128)(2,1)S(1)}, bf16[32,3584]{1,0:T(8,128)(2,1)S(1)}, u32[]{:S(2)}, u32[]{:S(2)}) %collective-permute-start.20) | collective-permute-done | bytes 229408 | tf_op jit(solution)/shard_map/ppermute | solution.py:68
  126.1 2.2 %collective-permute-done.18 = bf16[32,3584]{1,0:T(8,128)(2,1)S(1)} collective-permute-done((bf16[32,3584]{1,0:T(8,128)(2,1)S(1)}, bf16[32,3584]{1,0:T(8,128)(2,1)S(1)}, u32[]{:S(2)}, u32[]{:S(2)}) %collective-permute-start.18) | collective-permute-done | bytes 229408 | tf_op jit(solution)/shard_map/ppermute | solution.py:66
  (96 shorter events, 26.7 us)
Async XLA Ops:
  5.4 11.1 %collective-permute-start.3 = (bf16[32,3584]{1,0:T(8,128)(2,1)S(1)}, bf16[32,3584]{1,0:T(8,128)(2,1)S(1)}, u32[]{:S(2)}, u32[]{:S(2)}) collective-permute-start(bf16[32,3584]{1,0:T(8,128)(2,1)S(1)} %get-tuple-element.33), channel_id=1, source_target_pairs={{0,12},{1,13},{2,14},{3,15},{4,0},{5,1},{6,2},{7,3},{8,4},{9,5},{1... | collective-permute-start | bytes 688136 | tf_op jit(solution)/shard_map/ppermute | solution.py:33
  5.5 13.9 %collective-permute-start.2 = (bf16[32,3584]{1,0:T(8,128)(2,1)S(1)}, bf16[32,3584]{1,0:T(8,128)(2,1)S(1)}, u32[]{:S(2)}, u32[]{:S(2)}) collective-permute-start(bf16[32,3584]{1,0:T(8,128)(2,1)S(1)} %get-tuple-element.34), channel_id=1, source_target_pairs={{0,1},{1,2},{2,3},{3,0},{4,5},{5,6},{6,7},{7,4},{8,9},{9,10},{10,1... | collective-permute-start | bytes 688136 | tf_op jit(solution)/shard_map/ppermute | solution.py:34
  6.9 12.6 %collective-permute-start.1 = (bf16[32,3584]{1,0:T(8,128)(2,1)S(1)}, bf16[32,3584]{1,0:T(8,128)(2,1)S(1)}, u32[]{:S(2)}, u32[]{:S(2)}) collective-permute-start(bf16[32,3584]{1,0:T(8,128)(2,1)S(1)} %get-tuple-element.34), channel_id=1, source_target_pairs={{0,2},{1,3},{2,0},{3,1},{4,6},{5,7},{6,4},{7,5},{8,10},{9,11},{10,... | collective-permute-start | bytes 688136 | tf_op jit(solution)/shard_map/ppermute | solution.py:35
  16.6 22.6 %collective-permute-start.8 = (bf16[4,32,3584]{2,1,0:T(8,128)(2,1)S(1)}, bf16[4,32,3584]{2,1,0:T(8,128)(2,1)S(1)}, u32[]{:S(2)}, u32[]{:S(2)}) collective-permute-start(bf16[4,32,3584]{2,1,0:T(8,128)(2,1)S(1)} %get-tuple-element.29), channel_id=1, source_target_pairs={{0,3},{1,0},{2,1},{3,2},{4,7},{5,4},{6,5},{7,6},{8,11},{9,8},{10,9... | collective-permute-start | bytes 2752520 | tf_op jit(solution)/shard_map/ppermute | solution.py:23
  19.4 23.6 %collective-permute-start.9 = (bf16[4,32,3584]{2,1,0:T(8,128)(2,1)S(1)}, bf16[4,32,3584]{2,1,0:T(8,128)(2,1)S(1)}, u32[]{:S(2)}, u32[]{:S(2)}) collective-permute-start(bf16[4,32,3584]{2,1,0:T(8,128)(2,1)S(1)} %get-tuple-element.29), channel_id=1, source_target_pairs={{0,1},{1,2},{2,3},{3,0},{4,5},{5,6},{6,7},{7,4},{8,9},{9,10},{10,1... | collective-permute-start | bytes 2752520 | tf_op jit(solution)/shard_map/ppermute | solution.py:24
  19.6 23.7 %collective-permute-start.6 = (bf16[4,32,3584]{2,1,0:T(8,128)(2,1)S(1)}, bf16[4,32,3584]{2,1,0:T(8,128)(2,1)S(1)}, u32[]{:S(2)}, u32[]{:S(2)}) collective-permute-start(bf16[4,32,3584]{2,1,0:T(8,128)(2,1)S(1)} %get-tuple-element.27), channel_id=1, source_target_pairs={{0,12},{1,13},{2,14},{3,15},{4,0},{5,1},{6,2},{7,3},{8,4},{9,5},{1... | collective-permute-start | bytes 2752520 | tf_op jit(solution)/shard_map/ppermute | solution.py:23
  24.6 21.0 %collective-permute-start.7 = (bf16[4,32,3584]{2,1,0:T(8,128)(2,1)S(1)}, bf16[4,32,3584]{2,1,0:T(8,128)(2,1)S(1)}, u32[]{:S(2)}, u32[]{:S(2)}) collective-permute-start(bf16[4,32,3584]{2,1,0:T(8,128)(2,1)S(1)} %get-tuple-element.27), channel_id=1, source_target_pairs={{0,4},{1,5},{2,6},{3,7},{4,8},{5,9},{6,10},{7,11},{8,12},{9,13},{1... | collective-permute-start | bytes 2752520 | tf_op jit(solution)/shard_map/ppermute | solution.py:24
  39.3 19.8 %collective-permute-start.13 = (bf16[4,16,3584]{2,1,0:T(8,128)(2,1)S(1)}, bf16[4,16,3584]{2,1,0:T(8,128)(2,1)S(1)}, u32[]{:S(2)}, u32[]{:S(2)}) collective-permute-start(bf16[4,16,3584]{2,1,0:T(8,128)(2,1)S(1)} %slice.191), channel_id=1, source_target_pairs={{0,3},{1,0},{2,1},{3,2},{4,7},{5,4},{6,5},{7,6},{8,11},{9,8},{10,9... | collective-permute-start | bytes 1376264 | tf_op jit(solution)/shard_map/ppermute | solution.py:27
  43.1 16.1 %collective-permute-start.12 = (bf16[4,16,3584]{2,1,0:T(8,128)(2,1)S(1)}, bf16[4,16,3584]{2,1,0:T(8,128)(2,1)S(1)}, u32[]{:S(2)}, u32[]{:S(2)}) collective-permute-start(bf16[4,16,3584]{2,1,0:T(8,128)(2,1)S(1)} %slice.190), channel_id=1, source_target_pairs={{0,1},{1,2},{2,3},{3,0},{4,5},{5,6},{6,7},{7,4},{8,9},{9,10},{10,1... | collective-permute-start | bytes 1376264 | tf_op jit(solution)/shard_map/ppermute | solution.py:26
  43.4 15.8 %collective-permute-start.11 = (bf16[4,16,3584]{2,1,0:T(8,128)(2,1)S(1)}, bf16[4,16,3584]{2,1,0:T(8,128)(2,1)S(1)}, u32[]{:S(2)}, u32[]{:S(2)}) collective-permute-start(bf16[4,16,3584]{2,1,0:T(8,128)(2,1)S(1)} %slice.189), channel_id=1, source_target_pairs={{0,12},{1,13},{2,14},{3,15},{4,0},{5,1},{6,2},{7,3},{8,4},{9,5},{1... | collective-permute-start | bytes 1376264 | tf_op jit(solution)/shard_map/ppermute | solution.py:27
  45.6 13.6 %collective-permute-start.10 = (bf16[4,16,3584]{2,1,0:T(8,128)(2,1)S(1)}, bf16[4,16,3584]{2,1,0:T(8,128)(2,1)S(1)}, u32[]{:S(2)}, u32[]{:S(2)}) collective-permute-start(bf16[4,16,3584]{2,1,0:T(8,128)(2,1)S(1)} %slice.188), channel_id=1, source_target_pairs={{0,4},{1,5},{2,6},{3,7},{4,8},{5,9},{6,10},{7,11},{8,12},{9,13},{1... | collective-permute-start | bytes 1376264 | tf_op jit(solution)/shard_map/ppermute | solution.py:26
  55.7 45.2 %collective-permute-start.24 = (bf16[4,16,3584]{2,1,0:T(8,128)(2,1)S(1)}, bf16[4,16,3584]{2,1,0:T(8,128)(2,1)S(1)}, u32[]{:S(2)}, u32[]{:S(2)}) collective-permute-start(bf16[4,16,3584]{2,1,0:T(8,128)(2,1)S(1)} %slice.218), channel_id=1, source_target_pairs={{0,3},{1,0},{2,1},{3,2},{4,7},{5,4},{6,5},{7,6},{8,11},{9,8},{10,9... | collective-permute-start | bytes 1376264 | tf_op jit(solution)/shard_map/ppermute | solution.py:48
  59.1 43.9 %collective-permute-start.21 = (bf16[4,16,3584]{2,1,0:T(8,128)(2,1)S(1)}, bf16[4,16,3584]{2,1,0:T(8,128)(2,1)S(1)}, u32[]{:S(2)}, u32[]{:S(2)}) collective-permute-start(bf16[4,16,3584]{2,1,0:T(8,128)(2,1)S(1)} %slice.212), channel_id=1, source_target_pairs={{0,1},{1,2},{2,3},{3,0},{4,5},{5,6},{6,7},{7,4},{8,9},{9,10},{10,1... | collective-permute-start | bytes 1376264 | tf_op jit(solution)/shard_map/ppermute | solution.py:47
  63.9 16.5 %collective-permute-start.25 = (bf16[4,16,3584]{2,1,0:T(8,128)(2,1)S(1)}, bf16[4,16,3584]{2,1,0:T(8,128)(2,1)S(1)}, u32[]{:S(2)}, u32[]{:S(2)}) collective-permute-start(bf16[4,16,3584]{2,1,0:T(8,128)(2,1)S(1)} %get-tuple-element.25), channel_id=1, source_target_pairs={{0,1},{1,2},{2,3},{3,0},{4,5},{5,6},{6,7},{7,4},{8,9},{9,10},{10,1... | collective-permute-start | bytes 1376264 | tf_op jit(solution)/shard_map/ppermute | solution.py:45
  64.2 16.3 %collective-permute-start.22 = (bf16[4,16,3584]{2,1,0:T(8,128)(2,1)S(1)}, bf16[4,16,3584]{2,1,0:T(8,128)(2,1)S(1)}, u32[]{:S(2)}, u32[]{:S(2)}) collective-permute-start(bf16[4,16,3584]{2,1,0:T(8,128)(2,1)S(1)} %get-tuple-element.26), channel_id=1, source_target_pairs={{0,3},{1,0},{2,1},{3,2},{4,7},{5,4},{6,5},{7,6},{8,11},{9,8},{10,9... | collective-permute-start | bytes 1376264 | tf_op jit(solution)/shard_map/ppermute | solution.py:46
  67.6 19.5 %collective-permute-start.14 = (bf16[4,32,3584]{2,1,0:T(8,128)(2,1)S(1)}, bf16[4,32,3584]{2,1,0:T(8,128)(2,1)S(1)}, u32[]{:S(2)}, u32[]{:S(2)}) collective-permute-start(bf16[4,32,3584]{2,1,0:T(8,128)(2,1)S(1)} %pad_maximum_fusion.7), channel_id=1, source_target_pairs={{0,4},{1,5},{2,6},{3,7},{4,8},{5,9},{6,10},{7,11},{8,12},{9,13},{1... | collective-permute-start | bytes 2752520 | tf_op jit(solution)/shard_map/ppermute | solution.py:50
  80.4 20.3 %collective-permute-start.15 = (bf16[4,32,3584]{2,1,0:T(8,128)(2,1)S(1)}, bf16[4,32,3584]{2,1,0:T(8,128)(2,1)S(1)}, u32[]{:S(2)}, u32[]{:S(2)}) collective-permute-start(bf16[4,32,3584]{2,1,0:T(8,128)(2,1)S(1)} %pad_maximum_fusion.8), channel_id=1, source_target_pairs={{0,12},{1,13},{2,14},{3,15},{4,0},{5,1},{6,2},{7,3},{8,4},{9,5},{1... | collective-permute-start | bytes 2752520 | tf_op jit(solution)/shard_map/ppermute | solution.py:51
  80.5 22.4 %collective-permute-start.26 = (bf16[4,16,3584]{2,1,0:T(8,128)(2,1)S(1)}, bf16[4,16,3584]{2,1,0:T(8,128)(2,1)S(1)}, u32[]{:S(2)}, u32[]{:S(2)}) collective-permute-start(bf16[4,16,3584]{2,1,0:T(8,128)(2,1)S(1)} %add_convert_fusion), channel_id=1, source_target_pairs={{0,1},{1,2},{2,3},{3,0},{4,5},{5,6},{6,7},{7,4},{8,9},{9,10},{10,1... | collective-permute-start | bytes 1376264 | tf_op jit(solution)/shard_map/ppermute | solution.py:56
  87.1 15.8 %collective-permute-start.23 = (bf16[4,16,3584]{2,1,0:T(8,128)(2,1)S(1)}, bf16[4,16,3584]{2,1,0:T(8,128)(2,1)S(1)}, u32[]{:S(2)}, u32[]{:S(2)}) collective-permute-start(bf16[4,16,3584]{2,1,0:T(8,128)(2,1)S(1)} %add_convert_fusion.1), channel_id=1, source_target_pairs={{0,3},{1,0},{2,1},{3,2},{4,7},{5,4},{6,5},{7,6},{8,11},{9,8},{10,9... | collective-permute-start | bytes 1376264 | tf_op jit(solution)/shard_map/ppermute | solution.py:57
  100.7 13.3 %collective-permute-start.17 = (bf16[4,16,3584]{2,1,0:T(8,128)(2,1)S(1)}, bf16[4,16,3584]{2,1,0:T(8,128)(2,1)S(1)}, u32[]{:S(2)}, u32[]{:S(2)}) collective-permute-start(bf16[4,16,3584]{2,1,0:T(8,128)(2,1)S(1)} %add_convert_fusion.2), channel_id=1, source_target_pairs={{0,4},{1,5},{2,6},{3,7},{4,8},{5,9},{6,10},{7,11},{8,12},{9,13},{1... | collective-permute-start | bytes 1376264 | tf_op jit(solution)/shard_map/ppermute | solution.py:56
  100.8 17.1 %collective-permute-start.16 = (bf16[4,16,3584]{2,1,0:T(8,128)(2,1)S(1)}, bf16[4,16,3584]{2,1,0:T(8,128)(2,1)S(1)}, u32[]{:S(2)}, u32[]{:S(2)}) collective-permute-start(bf16[4,16,3584]{2,1,0:T(8,128)(2,1)S(1)} %add_convert_fusion.3), channel_id=1, source_target_pairs={{0,12},{1,13},{2,14},{3,15},{4,0},{5,1},{6,2},{7,3},{8,4},{9,5},{1... | collective-permute-start | bytes 1376264 | tf_op jit(solution)/shard_map/ppermute | solution.py:57
  103.3 17.3 %collective-permute-start.29 = (bf16[32,3584]{1,0:T(8,128)(2,1)S(1)}, bf16[32,3584]{1,0:T(8,128)(2,1)S(1)}, u32[]{:S(2)}, u32[]{:S(2)}) collective-permute-start(bf16[32,3584]{1,0:T(8,128)(2,1)S(1)} %get-tuple-element.23), channel_id=1, source_target_pairs={{0,8},{1,9},{2,10},{3,11},{4,12},{5,13},{6,14},{7,15},{8,0},{9,1},... | collective-permute-start | bytes 688136 | tf_op jit(solution)/shard_map/ppermute | solution.py:68
  103.5 17.2 %collective-permute-start.28 = (bf16[32,3584]{1,0:T(8,128)(2,1)S(1)}, bf16[32,3584]{1,0:T(8,128)(2,1)S(1)}, u32[]{:S(2)}, u32[]{:S(2)}) collective-permute-start(bf16[32,3584]{1,0:T(8,128)(2,1)S(1)} %get-tuple-element.24), channel_id=1, source_target_pairs={{0,12},{1,13},{2,14},{3,15},{4,0},{5,1},{6,2},{7,3},{8,4},{9,5},{1... | collective-permute-start | bytes 688136 | tf_op jit(solution)/shard_map/ppermute | solution.py:67
  105.5 15.1 %collective-permute-start.27 = (bf16[32,3584]{1,0:T(8,128)(2,1)S(1)}, bf16[32,3584]{1,0:T(8,128)(2,1)S(1)}, u32[]{:S(2)}, u32[]{:S(2)}) collective-permute-start(bf16[32,3584]{1,0:T(8,128)(2,1)S(1)} %get-tuple-element.22), channel_id=1, source_target_pairs={{0,4},{1,5},{2,6},{3,7},{4,8},{5,9},{6,10},{7,11},{8,12},{9,13},{1... | collective-permute-start | bytes 688136 | tf_op jit(solution)/shard_map/ppermute | solution.py:66
  (10 other events, 68.9 us)
